TPU v7x, 32 devices: a whole 2x2x4 slice. The times are simulated.
32 devices in a mesh: groups: 2 (over x), tm: 8 (over z, y), dp: 2 (over core).
Axes of the slice: x: 2, y: 2, z: 4, core: 2. Of those that a mesh axis runs over, the one named last changes fastest.
Arguments:
- clips: bfloat16 [4, 16, 32, 16, 256], P(('groups', 'dp'), 'tm'), parts along dimension 0, may hold values from -6 to 6
- kernel: bfloat16 [3, 3, 3, 256, 256], replicated, may hold values from -0.078125 to 0.078125
- cotangent: bfloat16 [4, 16, 32, 16, 256], P(('groups', 'dp'), 'tm'), parts along dimension 0, may hold values from -6 to 6
Outputs:
- output: bfloat16 [4, 16, 32, 16, 256], P(('groups', 'dp'), 'tm'), parts along dimension 0
- grad_input: bfloat16 [4, 16, 32, 16, 256], P(('groups', 'dp'), 'tm'), parts along dimension 0
- grad_kernel: float32 [6, 3, 3, 256, 256], P('groups', None, None, ('tm', 'dp')), parts along dimension 0
There are 2 independent parts, one for each index of `groups`. A program takes and returns all parts, laid end to end along the dimension named above; an argument that names none is the same for every part. Nothing has to cross between parts.
All inputs are finite; a program needn't handle non-finite values.
Results may differ from a plain program's by a relative error of at most 0.004.
Values may be sent and summed in bfloat16 or wider, within the bound.
No kernel may reach another device: no remote copies, remote signals or barrier semaphores. Data moves between devices by JAX's collectives and lax.ppermute only.
A program may use at most 128 MiB of HBM per device.

v0:
```python
import jax
import jax.numpy as jnp
from jax import lax
from jax.sharding import PartitionSpec as P


def passed_along(value, axis, steps):
    count = lax.axis_size(axis)
    leading, last = (max(0, -steps), min(count, count - steps))
    return lax.ppermute(value, axis, [(source, source + steps) for source in range(leading, last)])


def convolve(source, kernel, time_pad, flipped):
    if flipped:
        kernel = lax.rev(kernel, (0, 1, 2))
        layout = "DHWOI"
    else:
        layout = "DHWIO"
    return lax.conv_general_dilated(
        source,
        kernel,
        (1, 1, 1),
        [time_pad, (1, 1), (1, 1)],
        dimension_numbers=("NDHWC", layout, "NDHWC"),
        preferred_element_type=jnp.float32,
    )


def kernel_terms(extended, cotangent):
    frames = cotangent.shape[1]
    height = cotangent.shape[2]
    width = cotangent.shape[3]
    chans = cotangent.shape[4]
    spaced = jnp.pad(extended, ((0, 0), (0, 0), (1, 1), (1, 1), (0, 0)))
    flat_grad = cotangent.reshape(-1, chans)
    pieces = []
    for kt in range(3):
        for kh in range(3):
            for kw in range(3):
                window = spaced[:, kt : kt + frames, kh : kh + height, kw : kw + width, :].reshape(
                    -1, chans
                )
                pieces.append(
                    lax.dot_general(
                        window,
                        flat_grad,
                        (((0,), (0,)), ((), ())),
                        preferred_element_type=jnp.float32,
                    )
                )
    return jnp.stack(pieces).reshape(3, 3, 3, chans, chans)


def shards(clips, kernel, cotangent):
    frames = clips.shape[1]
    wide = clips.astype(jnp.float32)
    act = jax.nn.silu(wide).astype(jnp.bfloat16)
    earlier = passed_along(act, "tm", 1)
    extended = jnp.concatenate([earlier, act], axis=1)
    conv = convolve(extended, kernel, (0, 0), False)
    output = (wide + conv).astype(jnp.bfloat16)
    padded_grad = jnp.pad(cotangent, ((0, 0), (2, 2), (0, 0), (0, 0), (0, 0)))
    partial_grad = convolve(padded_grad, kernel, (0, 0), True)
    returned = passed_along(partial_grad[:, :2].astype(jnp.bfloat16), "tm", -1).astype(jnp.float32)
    returned = jnp.pad(returned, ((0, 0), (0, frames - 2), (0, 0), (0, 0), (0, 0)))
    grad_act = partial_grad[:, 2:] + returned
    sig = jax.nn.sigmoid(wide)
    grad_input = (
        cotangent.astype(jnp.float32) + grad_act * sig * (1.0 + wide * (1.0 - sig))
    ).astype(jnp.bfloat16)
    terms = kernel_terms(extended, cotangent)
    grad_kernel = lax.psum_scatter(terms, ("tm", "dp"), scatter_dimension=3, tiled=True)
    return (output, grad_input, grad_kernel)


def solution(mesh):
    in_specs = (
        P(("groups", "dp"), "tm", None, None, None),
        P(),
        P(("groups", "dp"), "tm", None, None, None),
    )
    out_specs = (
        P(("groups", "dp"), "tm", None, None, None),
        P(("groups", "dp"), "tm", None, None, None),
        P("groups", None, None, ("tm", "dp"), None),
    )
    return jax.shard_map(shards, mesh=mesh, in_specs=in_specs, out_specs=out_specs, check_vma=False)
```

profile of v0, /device:TPU:0, one launch (start us, length us, event | category | flops | bytes accessed | tf_op | source)
XLA Modules:
  0.0 156.7 jit_solution(10904354669497272502)
XLA Ops:
  7.2 0.0 copy-start
  7.2 0.0 reduce-scatter.2.cloned.1.call-start
  7.2 0.0 copy-start.2
  7.2 1.5 fusion.49
  8.8 4.9 %collective-permute-start = (bf16[1,2,32,16,256]{4,2,3,1,0:T(8,128)(2,1)S(1)}, bf16[1,2,32,16,256]{4,2,3,1,0:T(8,128)(2,1)S(1)}, u32[]{:S(2)}, u32[]{:S(2)}) collective-permute-start(bf16[1,2,32,16,256]{4,2,3,1,0:T(8,128)(2,1)S(1)} %fusion.49), channel_id=1, source_target_pairs={{0,2},{2,4},{4,6},{6,8},{8,10},{10,12},{12,14},{1,3},{3,5},{5,7},{... | collective-permute-start | bytes 1572872 | tf_op jit(solution)/shard_map/ppermute | solution.py:10
  13.7 11.1 %collective-permute-done = bf16[1,2,32,16,256]{4,2,3,1,0:T(8,128)(2,1)S(1)} collective-permute-done((bf16[1,2,32,16,256]{4,2,3,1,0:T(8,128)(2,1)S(1)}, bf16[1,2,32,16,256]{4,2,3,1,0:T(8,128)(2,1)S(1)}, u32[]{:S(2)}, u32[]{:S(2)}) %collective-permute-start) | collective-permute-done | bytes 524320 | tf_op jit(solution)/shard_map/ppermute | solution.py:10
  24.9 1.1 pad_maximum_fusion
  26.0 2.2 %fusion.45 = f32[27,256,256]{2,1,0:T(8,128)} fusion(bf16[1,4,32,16,256]{4,2,3,1,0:T(8,128)(2,1)S(1)} %get-tuple-element.9, bf16[2,32,16,256]{3,2,1,0:T(8,128)(2,1)} %bitcast.338), kind=kOutput, calls=%fused_computation.103 | convolution fusion | flops 134217728 | bytes 1835008 | tf_op jit(solution)/shard_map/dot_general | solution.py:44
  28.1 0.0 copy-done.2
  28.1 1.1 fusion.44
  29.3 1.1 fusion.43
  30.4 1.1 fusion.42
  31.5 1.1 fusion.41
  32.6 1.1 fusion.40
  33.7 1.1 fusion.39
  34.8 1.1 fusion.38
  36.0 1.1 fusion.37
  37.1 1.1 fusion.36
  38.2 1.1 fusion.35
  39.3 1.2 fusion.34
  40.5 1.1 fusion.33
  41.6 1.1 fusion.32
  42.8 1.1 fusion.31
  43.9 1.1 fusion.30
  45.0 1.1 fusion.29
  46.1 1.1 fusion.28
  47.3 1.1 fusion.27
  48.4 1.1 fusion.26
  49.5 1.1 fusion.25
  50.7 1.1 fusion.24
  51.8 0.0 copy-done.4
  51.8 1.3 fusion.23
  53.1 1.1 fusion.22
  54.2 1.1 fusion.21
  55.3 1.1 fusion.20
  56.5 1.1 fusion.19
  57.6 0.0 reduce-scatter.2.cloned.1.call-update
  57.6 1.2 copy.165
  58.8 0.1 pad.9
  58.9 0.4 copy.44
  59.3 0.1 slice.123
  59.5 0.0 copy-done
  59.5 0.0 copy-done.6
  59.5 12.9 %convolution_select_fusion = f32[4,32,8,3,256]{4,2,3,1,0:T(8,128)S(1)} fusion(bf16[3,3,3,256,256]{4,3,2,1,0:T(8,128)(2,1)S(1)} %copy-done, pred[8,3]{0,1:T(4,128)(4,1)S(1)} %copy-done.6, bf16[2,32,1,7,2,256]{5,3,4,1,0,2:T(8,128)(2,1)S(1)} %slice.123, bf16[2,32,1,8,3,256]{5,3,4,1,0,2:T(8,128)(2,1)S(1)} %copy.44), kind=kOutput, calls=%fused_computation.34 | convolution fusion | flops 5327290368 | bytes 7929880 | tf_op jit(solution)/shard_map/conv_general_dilated | solution.py:19
  72.4 0.0 copy-start.1
  72.4 0.1 slice.248
  72.5 0.2 copy.46
  72.8 1.6 %collective-permute-start.1 = (bf16[1,2,32,16,256]{4,2,3,1,0:T(8,128)(2,1)S(1)}, bf16[1,2,32,16,256]{4,2,3,1,0:T(8,128)(2,1)S(1)}, u32[]{:S(2)}, u32[]{:S(2)}) collective-permute-start(bf16[1,2,32,16,256]{4,2,3,1,0:T(8,128)(2,1)S(1)} %slice_bitcast_fusion.2), channel_id=1, source_target_pairs={{2,0},{4,2},{6,4},{8,6},{10,8},{12,10},{14,12},{3,1},{5,3},{7,5},{... | collective-permute-start | bytes 1572872 | tf_op jit(solution)/shard_map/ppermute | solution.py:10
  74.4 0.1 slice.124
  74.5 0.5 copy.45
  75.0 0.0 copy-done.1
  75.0 0.2 pad.7
  75.2 0.9 copy.39
  76.1 0.2 slice.121
  76.4 0.0 copy-start.3
  76.4 0.0 copy-start.5
  76.4 6.1 %fusion.9 = f32[2,32,8,3,256]{4,2,3,1,0:T(8,128)S(1)} fusion(bf16[3,3,3,256,256]{4,3,2,1,0:T(8,128)(2,1)S(1)} %copy-done, bf16[4,32,1,7,2,256]{5,3,4,1,0,2:T(8,128)(2,1)S(1)} %slice.121, bf16[4,32,1,8,3,256]{5,3,4,1,0,2:T(8,128)(2,1)S(1)} %copy.39, pred[8,3]{0,1:T(4,128)(4,1)S(1)} %copy-done.6), kind=kOutput, calls=%fused_computation.40 | convolution fusion | flops 5330829312 | bytes 7602200 | tf_op jit(solution)/shard_map/conv_general_dilated | solution.py:19
  82.5 0.5 copy.40
  83.0 5.3 %collective-permute-done.1 = bf16[1,2,32,16,256]{4,2,3,1,0:T(8,128)(2,1)S(1)} collective-permute-done((bf16[1,2,32,16,256]{4,2,3,1,0:T(8,128)(2,1)S(1)}, bf16[1,2,32,16,256]{4,2,3,1,0:T(8,128)(2,1)S(1)}, u32[]{:S(2)}, u32[]{:S(2)}) %collective-permute-start.1) | collective-permute-done | bytes 524320 | tf_op jit(solution)/shard_map/ppermute | solution.py:10
  88.3 0.0 copy-done.3
  88.3 0.8 fusion.54
  89.2 1.1 copy.75
  90.3 1.1 copy.74
  91.3 58.5 %reduce-scatter.2.cloned.1.call-done = f32[3,3,3,16,256]{4,3,2,1,0:T(8,128)} async-done(((f32[3,3,3,256,256]{4,3,2,1,0:T(8,128)}), f32[3,3,3,16,256]{4,3,2,1,0:T(8,128)}) %reduce-scatter.2.cloned.1.call-update) | async-done | bytes 442384 | tf_op jit(solution)/shard_map/reduce_scatter | solution.py:72
  (4 shorter events, 0.0 us)
Async XLA Ops:
  7.2 52.3 %copy-start = (bf16[3,3,3,256,256]{4,3,2,1,0:T(8,128)(2,1)S(1)}, bf16[3,3,3,256,256]{4,3,2,1,0:T(8,128)(2,1)}, u32[]{:S(2)}) copy-start(bf16[3,3,3,256,256]{4,3,2,1,0:T(8,128)(2,1)} %param.4) | copy-start | bytes 10616836
  7.2 142.7 %reduce-scatter.2.cloned.1.call-start = ((), (), s32[]{:S(2)}) async-start(), calls=%async_computation.1 | async-start | bytes 7520256 | tf_op jit(solution)/shard_map/reduce_scatter | solution.py:72
  7.2 20.9 %copy-start.2 = (bf16[1,2,32,16,256]{4,3,2,1,0:T(8,128)(2,1)S(1)}, bf16[1,2,32,16,256]{4,3,2,1,0:T(8,128)(2,1)}, u32[]{:S(2)}) copy-start(bf16[1,2,32,16,256]{4,3,2,1,0:T(8,128)(2,1)} %param.5) | copy-start | bytes 1572868
  8.8 16.1 %collective-permute-start = (bf16[1,2,32,16,256]{4,2,3,1,0:T(8,128)(2,1)S(1)}, bf16[1,2,32,16,256]{4,2,3,1,0:T(8,128)(2,1)S(1)}, u32[]{:S(2)}, u32[]{:S(2)}) collective-permute-start(bf16[1,2,32,16,256]{4,2,3,1,0:T(8,128)(2,1)S(1)} %fusion.49), channel_id=1, source_target_pairs={{0,2},{2,4},{4,6},{6,8},{8,10},{10,12},{12,14},{1,3},{3,5},{5,7},{... | collective-permute-start | bytes 1572872 | tf_op jit(solution)/shard_map/ppermute | solution.py:10
  47.3 4.5 %copy-start.4 = (bf16[1,2,32,16,256]{4,3,2,1,0:T(8,128)(2,1)S(1)}, bf16[1,2,32,16,256]{4,3,2,1,0:T(8,128)(2,1)}, u32[]{:S(2)}) copy-start(bf16[1,2,32,16,256]{4,3,2,1,0:T(8,128)(2,1)} %param.3) | copy-start | bytes 1572868
  56.5 3.0 %copy-start.6 = (pred[8,3]{0,1:T(4,128)(4,1)S(1)}, pred[8,3]{0,1:T(4,128)(4,1)}, u32[]{:S(2)}) copy-start(pred[8,3]{0,1:T(4,128)(4,1)} %constant.19) | copy-start | bytes 76
  72.4 2.6 %copy-start.1 = (bf16[4,32,1,16,256]{4,1,3,0,2:T(8,128)(2,1)S(1)}, bf16[4,32,1,16,256]{4,1,3,0,2:T(8,128)(2,1)}, u32[]{:S(2)}) copy-start(bf16[4,32,1,16,256]{4,1,3,0,2:T(8,128)(2,1)} %get-tuple-element.10) | copy-start | bytes 3145732
  72.8 15.6 %collective-permute-start.1 = (bf16[1,2,32,16,256]{4,2,3,1,0:T(8,128)(2,1)S(1)}, bf16[1,2,32,16,256]{4,2,3,1,0:T(8,128)(2,1)S(1)}, u32[]{:S(2)}, u32[]{:S(2)}) collective-permute-start(bf16[1,2,32,16,256]{4,2,3,1,0:T(8,128)(2,1)S(1)} %slice_bitcast_fusion.2), channel_id=1, source_target_pairs={{2,0},{4,2},{6,4},{8,6},{10,8},{12,10},{14,12},{3,1},{5,3},{7,5},{... | collective-permute-start | bytes 1572872 | tf_op jit(solution)/shard_map/ppermute | solution.py:10
  76.4 12.0 %copy-start.3 = (bf16[1,2,32,16,256]{4,3,2,1,0:T(8,128)(2,1)S(1)}, bf16[1,2,32,16,256]{4,3,2,1,0:T(8,128)(2,1)}, u32[]{:S(2)}) copy-start(bf16[1,2,32,16,256]{4,3,2,1,0:T(8,128)(2,1)} %param.5) | copy-start | bytes 1572868
  76.4 12.0 %copy-start.5 = (bf16[1,2,32,16,256]{4,3,2,1,0:T(8,128)(2,1)S(1)}, bf16[1,2,32,16,256]{4,3,2,1,0:T(8,128)(2,1)}, u32[]{:S(2)}) copy-start(bf16[1,2,32,16,256]{4,3,2,1,0:T(8,128)(2,1)} %param.3) | copy-start | bytes 1572868
Sparse Core Ops, SparseCore 0:
  57.7 92.0 reduce-scatter.1
where the time goes:
time: 157 us
  waiting for transfers between devices  75 us (48%)
  matrix products  50.7 us (32%)
  between operations  14.2 us (9%)
  local copies, waits for them, and re-layouts  6.74 us (4%)
  starting transfers between devices  6.61 us (4%)
  other arithmetic  3.48 us (2%)
    reduce_scatter x1, waiting for transfers between devices, shards(): lax.psum_scatter(terms, ('tm', 'dp'), scatter_dimension=3, tiled=True)  58.5 us
    dot_general x27, matrix products, kernel_terms(): lax.dot_general(window, flat_grad, (((0,), (0,)), ((), ())), preferred_el...  31.6 us
    conv_general_dilated x2, matrix products, convolve(): lax.conv_general_dilated(source, kernel, (1, 1, 1), [time_pad, (1, 1), (1...  19.1 us
    ppermute x2, waiting for transfers between devices, passed_along(): lax.ppermute(value, axis, [(source, source + steps) for source in range(l...  16.5 us
    ppermute x2, starting transfers between devices, passed_along(): lax.ppermute(value, axis, [(source, source + steps) for source in range(l...  6.58 us
    unnamed x18, local copies, waits for them, and re-layouts  3.49 us
  transfers between devices with their start and end apart: 3, of which 3 were waited for; matrix products, arithmetic and copies ran while one was open for 17% of the time, Pallas kernels for 0%

commit v1 on v0

v1 whole, which is shorter than its diff:
```python
import jax
import jax.numpy as jnp
from jax import lax
from jax.sharding import PartitionSpec as P


def passed_along(value, axis, steps):
    count = lax.axis_size(axis)
    leading, last = (max(0, -steps), min(count, count - steps))
    return lax.ppermute(value, axis, [(source, source + steps) for source in range(leading, last)])


def swapped(value, axis):
    count = lax.axis_size(axis)
    return lax.ppermute(value, axis, [(source, count - 1 - source) for source in range(count)])


def convolve(source, kernel, flipped):
    if flipped:
        kernel = lax.rev(kernel, (0, 1, 2))
        layout = "DHWOI"
    else:
        layout = "DHWIO"
    return lax.conv_general_dilated(
        source,
        kernel,
        (1, 1, 1),
        [(0, 0), (1, 1), (1, 1)],
        dimension_numbers=("NDHWC", layout, "NDHWC"),
        preferred_element_type=jnp.float32,
    )


def kernel_terms(extended, cotangent):
    terms = lax.conv_general_dilated(
        extended,
        cotangent,
        (1, 1, 1),
        [(0, 0), (1, 1), (1, 1)],
        dimension_numbers=("CDHWN", "IDHWO", "NDHWC"),
        preferred_element_type=jnp.float32,
    )
    return jnp.transpose(terms, (1, 2, 3, 0, 4))


def channel_half(value, half, owners, pair):
    shape = value.shape
    split = value.reshape(shape[:-1] + (owners, pair, shape[-1] // (owners * pair)))
    taken = lax.dynamic_index_in_dim(split, half, axis=len(shape), keepdims=False)
    return taken.reshape(shape[:-1] + (owners * shape[-1] // (owners * pair),))


def shards(clips, kernel, cotangent):
    owners = lax.axis_size("tm")
    pair = lax.axis_size("dp")
    chans = clips.shape[-1]
    me = lax.axis_index("dp")
    wide = clips.astype(jnp.float32)
    act = jax.nn.silu(wide).astype(jnp.bfloat16)
    earlier = passed_along(act, "tm", 1)
    extended = jnp.concatenate([earlier, act], axis=1)
    following = passed_along(cotangent, "tm", -1)

    mine = channel_half(extended, me, owners, pair)
    theirs_for_me = swapped(channel_half(extended, pair - 1 - me, owners, pair), "dp")
    partner_cot = swapped(cotangent, "dp")
    both_ext = jnp.concatenate([mine, theirs_for_me], axis=0)
    both_cot = jnp.concatenate([cotangent, partner_cot], axis=0)
    terms = kernel_terms(both_ext, both_cot)
    terms = terms.reshape(terms.shape[:3] + (owners, chans // (owners * pair), chans))
    grad_kernel = lax.psum_scatter(terms, "tm", scatter_dimension=3, tiled=True)
    grad_kernel = grad_kernel.reshape(grad_kernel.shape[:3] + (chans // (owners * pair), chans))

    conv = convolve(extended, kernel, False)
    output = (wide + conv).astype(jnp.bfloat16)
    cot_ext = jnp.concatenate([cotangent, following], axis=1)
    grad_act = convolve(cot_ext, kernel, True)
    sig = jax.nn.sigmoid(wide)
    grad_input = (
        cotangent.astype(jnp.float32) + grad_act * sig * (1.0 + wide * (1.0 - sig))
    ).astype(jnp.bfloat16)
    return (output, grad_input, grad_kernel)


def solution(mesh):
    in_specs = (
        P(("groups", "dp"), "tm", None, None, None),
        P(),
        P(("groups", "dp"), "tm", None, None, None),
    )
    out_specs = (
        P(("groups", "dp"), "tm", None, None, None),
        P(("groups", "dp"), "tm", None, None, None),
        P("groups", None, None, ("tm", "dp"), None),
    )
    return jax.shard_map(shards, mesh=mesh, in_specs=in_specs, out_specs=out_specs, check_vma=False)
```

time: 157 us -> 167 us (1.064)
  local copies, waits for them, and re-layouts: 6.74 us -> 35.9 us
  matrix products: 50.7 us -> 27.8 us
  other arithmetic: 3.48 us -> 5.87 us
    dot_general x27 -> x0, matrix products: 31.6 us -> none  [kernel_terms(): lax.dot_general(window, flat_grad, (((0,), (0,)), ((), ())), preferred_el...]
    transpose x0 -> x1, matrix products: none -> 15.3 us  [kernel_terms(): return jnp.transpose(terms, (1, 2, 3, 0, 4))]
    reshape x0 -> x3, local copies, waits for them, and re-layouts: none -> 9.2 us  [the longest x2 7.08 us: channel_half(): return taken.reshape(shape[:-1] + (owners * shape[-1] // (owners * pair),))]
    conv_general_dilated x2, matrix products: 19.1 us -> 12.6 us  [convolve(): lax.conv_general_dilated(source, kernel, (1, 1, 1), [(0, 0), (1, 1), (1,...]
    concatenate x1 -> x2, local copies, waits for them, and re-layouts: 0.2 us -> 5.99 us  [shards(): extended = jnp.concatenate([earlier, act], axis=1)]
    dynamic_slice x0 -> x1, local copies, waits for them, and re-layouts: none -> 5.78 us  [channel_half(): lax.dynamic_index_in_dim(split, half, axis=len(shape), keepdims=False)]
    ppermute x2, waiting for transfers between devices: 16.5 us -> 21.8 us  [passed_along(): lax.ppermute(value, axis, [(source, source + steps) for source in range(l...]
    reduce_scatter x1, waiting for transfers between devices: 58.5 us -> 54 us  [shards(): grad_kernel = lax.psum_scatter(terms, 'tm', scatter_dimension=3, tiled=True)]
  transfers between devices with their start and end apart: 3 -> 5, of which waited for: 3 -> 3; matrix products, arithmetic and copies ran while one was open for 17% -> 28% of each run, Pallas kernels for 0% -> 0%
where the time goes in v1:
time: 167 us
  waiting for transfers between devices  75.8 us (45%)
  local copies, waits for them, and re-layouts  35.9 us (21%)
  matrix products  27.8 us (17%)
  between operations  14.2 us (9%)
  starting transfers between devices  7.07 us (4%)
  other arithmetic  5.87 us (4%)
    reduce_scatter x1, waiting for transfers between devices, shards(): grad_kernel = lax.psum_scatter(terms, 'tm', scatter_dimension=3, tiled=True)  54 us
    ppermute x2, waiting for transfers between devices, passed_along(): lax.ppermute(value, axis, [(source, source + steps) for source in range(l...  21.8 us
    transpose x1, matrix products, kernel_terms(): return jnp.transpose(terms, (1, 2, 3, 0, 4))  15.3 us
    conv_general_dilated x2, matrix products, convolve(): lax.conv_general_dilated(source, kernel, (1, 1, 1), [(0, 0), (1, 1), (1,...  12.6 us
    unnamed x16, local copies, waits for them, and re-layouts  7.29 us
    reshape x2, local copies, waits for them, and re-layouts, channel_half(): return taken.reshape(shape[:-1] + (owners * shape[-1] // (owners * pair),))  7.08 us
    ppermute x2, starting transfers between devices, passed_along(): lax.ppermute(value, axis, [(source, source + steps) for source in range(l...  7.03 us
    concatenate x2, local copies, waits for them, and re-layouts, shards(): extended = jnp.concatenate([earlier, act], axis=1)  5.99 us
  transfers between devices with their start and end apart: 5, of which 3 were waited for; matrix products, arithmetic and copies ran while one was open for 28% of the time, Pallas kernels for 0%

profile of v1, /device:TPU:0, one launch (start us, length us, event | category | flops | bytes accessed | tf_op | source)
XLA Modules:
  0.0 166.7 jit_solution(13373394352433095278)
XLA Ops:
  7.2 0.0 copy-start
  7.2 0.0 reduce-scatter.2.cloned.1.call-start
  7.2 2.3 %fusion.27 = bf16[1,2,32,16,256]{4,2,3,1,0:T(8,128)(2,1)} fusion(bf16[1,2,32,16,256]{4,3,2,1,0:T(8,128)(2,1)} %param.3), kind=kLoop, calls=%fused_computation.26 | loop fusion | flops 1572864 | bytes 1048576 | tf_op jit(solution)/shard_map/convert_element_type | solution.py:59
  9.5 5.7 %collective-permute-start = (bf16[1,2,32,16,256]{4,2,3,1,0:T(8,128)(2,1)}, bf16[1,2,32,16,256]{4,2,3,1,0:T(8,128)(2,1)}, u32[]{:S(2)}, u32[]{:S(2)}) collective-permute-start(bf16[1,2,32,16,256]{4,2,3,1,0:T(8,128)(2,1)} %fusion.27), channel_id=1, source_target_pairs={{0,2},{2,4},{4,6},{6,8},{8,10},{10,12},{12,14},{1,3},{3,5},{5,7},{... | collective-permute-start | bytes 1572872 | tf_op jit(solution)/shard_map/ppermute | solution.py:10
  15.3 0.0 collective-permute-start.3
  15.3 10.6 %collective-permute-done = bf16[1,2,32,16,256]{4,2,3,1,0:T(8,128)(2,1)} collective-permute-done((bf16[1,2,32,16,256]{4,2,3,1,0:T(8,128)(2,1)}, bf16[1,2,32,16,256]{4,2,3,1,0:T(8,128)(2,1)}, u32[]{:S(2)}, u32[]{:S(2)}) %collective-permute-start) | collective-permute-done | bytes 524320 | tf_op jit(solution)/shard_map/ppermute | solution.py:10
  25.9 2.8 %pad_maximum_fusion = (bf16[1,4,32,16,256]{4,2,3,1,0:T(8,128)(2,1)}, bf16[4,32,1,16,256]{4,1,3,0,2:T(8,128)(2,1)}) fusion(bf16[1,2,32,16,256]{4,2,3,1,0:T(8,128)(2,1)} %fusion.27, bf16[1,2,32,16,256]{4,2,3,1,0:T(8,128)(2,1)} %collective-permute-done), kind=kLoop, calls=%fused_computation.35 | loop fusion | flops 524288 | bytes 3145728 | tf_op jit(solution)/shard_map/concatenate | solution.py:61
  28.7 4.6 %copy.39 = bf16[1,4,32,16,256]{2,4,3,1,0:T(8,128)(2,1)} copy(bf16[1,4,32,16,256]{4,2,3,1,0:T(8,128)(2,1)} %get-tuple-element.11) | data formatting | bytes 2097152 | tf_op jit(solution)/shard_map/concatenate | solution.py:61
  33.3 5.8 %constant_dynamic-slice_fusion.1 = (bf16[1,4,32,16,8,1,16]{2,6,5,4,3,1,0:T(8,128)(2,1)}, bf16[1,4,32,16,8,1,16]{2,6,5,4,3,1,0:T(8,128)(2,1)}) fusion(bf16[1,4,32,16,8,2,16]{2,6,5,4,3,1,0:T(8,128)(2,1)} %bitcast.35, s32[]{:T(128)S(6)} %select_n.7, s32[]{:T(128)S(6)} %select_n.8), kind=kLoop, calls=%fused_computation.41 | loop fusion | bytes 2097160 | tf_op jit(solution)/shard_map/jit(dynamic_index_in_dim)/dynamic_slice | solution.py:49
  39.0 2.7 %copy.40 = bf16[1,4,32,16,128]{4,3,2,1,0:T(8,128)(2,1)} copy(bf16[1,4,32,16,128]{2,4,3,1,0:T(8,128)(2,1)} %bitcast.36) | data formatting | bytes 1048576 | tf_op jit(solution)/shard_map/reshape | solution.py:50
  41.7 0.0 collective-permute-start.2
  41.7 3.2 %copy.43 = bf16[1,2,32,16,256]{4,0,3,2,1:T(2,128)(2,1)} copy(bf16[1,2,32,16,256]{4,3,2,1,0:T(8,128)(2,1)} %param.5) | data formatting | bytes 1048576 | tf_op args[2]
  44.9 4.4 %copy.41 = bf16[1,4,32,16,128]{4,0,3,2,1:T(2,128)(2,1)} copy(bf16[1,4,32,16,128]{2,4,3,1,0:T(8,128)(2,1)} %bitcast.37) | data formatting | bytes 1048576 | tf_op jit(solution)/shard_map/reshape | solution.py:50
  49.3 0.0 copy-start.3
  49.3 0.0 copy-start.4
  49.3 0.0 collective-permute-done.3
  49.3 2.3 %copy.44 = bf16[1,2,32,16,256]{4,0,3,2,1:T(2,128)(2,1)S(1)} copy(bf16[1,2,32,16,256]{4,3,2,1,0:T(8,128)(2,1)} %collective-permute-done.3) | data formatting | bytes 1048576 | tf_op jit(solution)/shard_map/ppermute | solution.py:15
  51.7 0.0 collective-permute-done.2
  51.7 1.9 %copy.42 = bf16[1,4,32,16,128]{4,0,3,2,1:T(2,128)(2,1)S(1)} copy(bf16[1,4,32,16,128]{4,3,2,1,0:T(8,128)(2,1)} %collective-permute-done.2) | data formatting | bytes 1048576 | tf_op jit(solution)/shard_map/ppermute | solution.py:15
  53.6 0.0 copy-done.3
  53.6 0.0 copy-done.4
  53.6 15.3 %fusion.34 = f32[3,3,3,128,256]{4,3,2,1,0:T(8,128)S(1)} fusion(bf16[1,2,32,16,256]{4,0,3,2,1:T(2,128)(2,1)S(1)} %copy.44, bf16[1,2,32,16,256]{4,0,3,2,1:T(2,128)(2,1)S(1)} %copy-done.4, bf16[1,4,32,16,128]{4,0,3,2,1:T(2,128)(2,1)S(1)} %copy.42, bf16[1,4,32,16,128]{4,0,3,2,1:T(2,128)(2,1)S(1)} %copy-done.3), kind=kOutput, calls=%fused_computation.39 | convolution fusion | flops 3404726272 | bytes 5636096 | tf_op jit(solution)/shard_map/transpose | solution.py:43
  68.9 2.1 %copy.45 = f32[3,3,3,8,16,256]{5,4,2,1,0,3:T(8,128)} copy(f32[3,3,3,8,16,256]{5,4,3,2,1,0:T(8,128)S(1)} %bitcast.42) | data formatting | bytes 7077888 | tf_op jit(solution)/shard_map/reshape | solution.py:70
  71.0 0.0 reduce-scatter.2.cloned.1.call-update
  71.0 1.2 copy.33
  72.2 1.3 collective-permute-start.1
  73.5 1.4 pad
  74.9 0.0 copy-start.5
  75.0 0.9 copy.31
  75.9 0.2 slice.4
  76.1 0.0 copy-done
  76.1 0.0 copy-done.5
  76.1 6.1 %fusion.19 = f32[2,32,8,3,256]{4,2,3,1,0:T(8,128)S(1)} fusion(bf16[3,3,3,256,256]{4,3,2,1,0:T(8,128)(2,1)S(1)} %copy-done, bf16[4,32,1,7,2,256]{5,3,4,1,0,2:T(8,128)(2,1)S(1)} %slice.4, bf16[4,32,1,8,3,256]{5,3,4,1,0,2:T(8,128)(2,1)S(1)} %copy.31, pred[8,3]{0,1:T(4,128)(4,1)S(1)} %copy-done.5), kind=kOutput, calls=%fused_computation.20 | convolution fusion | flops 5330829312 | bytes 7602200 | tf_op jit(solution)/shard_map/conv_general_dilated | solution.py:24
  82.3 0.5 copy.32
  82.7 11.2 %collective-permute-done.1 = bf16[1,2,32,16,256]{4,2,3,1,0:T(8,128)(2,1)S(1)} collective-permute-done((bf16[1,2,32,16,256]{4,2,3,1,0:T(8,128)(2,1)S(1)}, bf16[1,2,32,16,256]{4,2,3,1,0:T(8,128)(2,1)S(1)}, u32[]{:S(2)}, u32[]{:S(2)}) %collective-permute-start.1) | collective-permute-done | bytes 524320 | tf_op jit(solution)/shard_map/ppermute | solution.py:10
  93.9 0.1 maximum_bitcast_fusion
  94.0 0.2 pad.2
  94.2 0.9 copy.37
  95.2 0.2 slice.6
  95.4 6.4 %fusion.16 = f32[2,32,8,3,256]{4,2,3,1,0:T(8,128)S(1)} fusion(bf16[3,3,3,256,256]{4,3,2,1,0:T(8,128)(2,1)S(1)} %copy-done, bf16[4,32,1,7,2,256]{5,3,4,1,0,2:T(8,128)(2,1)S(1)} %slice.6, bf16[4,32,1,8,3,256]{5,3,4,1,0,2:T(8,128)(2,1)S(1)} %copy.37, pred[8,3]{0,1:T(4,128)(4,1)S(1)} %copy-done.5), kind=kOutput, calls=%fused_computation.19 | convolution fusion | flops 5330829312 | bytes 7602200 | tf_op jit(solution)/shard_map/conv_general_dilated | solution.py:24
  101.8 0.0 copy-start.1
  101.8 0.0 copy-start.2
  101.9 0.5 copy.38
  102.3 0.5 copy-done.1
  102.9 0.2 copy-done.2
  103.0 0.7 fusion.32
  103.7 1.1 copy.46
  104.8 1.1 copy.47
  105.9 54.0 %reduce-scatter.2.cloned.1.call-done = f32[3,3,3,1,16,256]{5,4,2,1,0,3:T(8,128)} async-done(((f32[3,3,3,8,16,256]{5,4,2,1,0,3:T(8,128)}), f32[3,3,3,1,16,256]{5,4,2,1,0,3:T(8,128)}) %reduce-scatter.2.cloned.1.call-update) | async-done | bytes 442384 | tf_op jit(solution)/shard_map/reduce_scatter | solution.py:71
Async XLA Ops:
  7.2 68.9 %copy-start = (bf16[3,3,3,256,256]{4,3,2,1,0:T(8,128)(2,1)S(1)}, bf16[3,3,3,256,256]{4,3,2,1,0:T(8,128)(2,1)}, u32[]{:S(2)}) copy-start(bf16[3,3,3,256,256]{4,3,2,1,0:T(8,128)(2,1)} %param.4) | copy-start | bytes 10616836
  7.2 152.7 %reduce-scatter.2.cloned.1.call-start = ((), (), s32[]{:S(2)}) async-start(), calls=%async_computation.1 | async-start | bytes 3981312 | tf_op jit(solution)/shard_map/reduce_scatter | solution.py:71
  9.5 16.4 %collective-permute-start = (bf16[1,2,32,16,256]{4,2,3,1,0:T(8,128)(2,1)}, bf16[1,2,32,16,256]{4,2,3,1,0:T(8,128)(2,1)}, u32[]{:S(2)}, u32[]{:S(2)}) collective-permute-start(bf16[1,2,32,16,256]{4,2,3,1,0:T(8,128)(2,1)} %fusion.27), channel_id=1, source_target_pairs={{0,2},{2,4},{4,6},{6,8},{8,10},{10,12},{12,14},{1,3},{3,5},{5,7},{... | collective-permute-start | bytes 1572872 | tf_op jit(solution)/shard_map/ppermute | solution.py:10
  15.3 34.0 %collective-permute-start.3 = (bf16[1,2,32,16,256]{4,3,2,1,0:T(8,128)(2,1)}, bf16[1,2,32,16,256]{4,3,2,1,0:T(8,128)(2,1)}, u32[]{:S(2)}, u32[]{:S(2)}) collective-permute-start(bf16[1,2,32,16,256]{4,3,2,1,0:T(8,128)(2,1)} %param.5), channel_id=1, source_target_pairs={{0,1},{1,0},{2,3},{3,2},{4,5},{5,4},{6,7},{7,6},{8,9},{9,8},{10,11... | collective-permute-start | bytes 1572872 | tf_op jit(solution)/shard_map/ppermute | solution.py:15
  41.7 9.9 %collective-permute-start.2 = (bf16[1,4,32,16,128]{4,3,2,1,0:T(8,128)(2,1)}, bf16[1,4,32,16,128]{4,3,2,1,0:T(8,128)(2,1)}, u32[]{:S(2)}, u32[]{:S(2)}) collective-permute-start(bf16[1,4,32,16,128]{4,3,2,1,0:T(8,128)(2,1)} %copy.40), channel_id=1, source_target_pairs={{0,1},{1,0},{2,3},{3,2},{4,5},{5,4},{6,7},{7,6},{8,9},{9,8},{10,11... | collective-permute-start | bytes 1572872 | tf_op jit(solution)/shard_map/ppermute | solution.py:15
  49.3 4.3 %copy-start.3 = (bf16[1,4,32,16,128]{4,0,3,2,1:T(2,128)(2,1)S(1)}, bf16[1,4,32,16,128]{4,0,3,2,1:T(2,128)(2,1)}, u32[]{:S(2)}) copy-start(bf16[1,4,32,16,128]{4,0,3,2,1:T(2,128)(2,1)} %copy.41) | copy-start | bytes 1572868
  49.3 4.3 %copy-start.4 = (bf16[1,2,32,16,256]{4,0,3,2,1:T(2,128)(2,1)S(1)}, bf16[1,2,32,16,256]{4,0,3,2,1:T(2,128)(2,1)}, u32[]{:S(2)}) copy-start(bf16[1,2,32,16,256]{4,0,3,2,1:T(2,128)(2,1)} %copy.43) | copy-start | bytes 1572868
  72.2 21.7 %collective-permute-start.1 = (bf16[1,2,32,16,256]{4,2,3,1,0:T(8,128)(2,1)S(1)}, bf16[1,2,32,16,256]{4,2,3,1,0:T(8,128)(2,1)S(1)}, u32[]{:S(2)}, u32[]{:S(2)}) collective-permute-start(bf16[1,2,32,16,256]{4,2,3,1,0:T(8,128)(2,1)S(1)} %copy.33), channel_id=1, source_target_pairs={{2,0},{4,2},{6,4},{8,6},{10,8},{12,10},{14,12},{3,1},{5,3},{7,5},{... | collective-permute-start | bytes 1572872 | tf_op jit(solution)/shard_map/ppermute | solution.py:10
  74.9 1.2 copy-start.5
  101.8 1.0 copy-start.1
  101.8 1.2 copy-start.2
Sparse Core Ops, SparseCore 0:
  71.1 88.6 reduce-scatter.1

commit v2 on v1

v2 whole, which is shorter than its diff:
```python
import jax
import jax.numpy as jnp
from jax import lax
from jax.sharding import PartitionSpec as P


def passed_along(value, axis, steps):
    count = lax.axis_size(axis)
    leading, last = (max(0, -steps), min(count, count - steps))
    return lax.ppermute(value, axis, [(source, source + steps) for source in range(leading, last)])


def convolve(source, kernel, flipped):
    if flipped:
        kernel = lax.rev(kernel, (0, 1, 2))
        layout = "DHWOI"
    else:
        layout = "DHWIO"
    return lax.conv_general_dilated(
        source,
        kernel,
        (1, 1, 1),
        [(0, 0), (1, 1), (1, 1)],
        dimension_numbers=("NDHWC", layout, "NDHWC"),
        preferred_element_type=jnp.float32,
    )


def kernel_terms(extended, cotangent):
    frames, height, width, chans = cotangent.shape[1:]
    spaced = jnp.pad(extended, ((0, 0), (0, 0), (1, 1), (1, 1), (0, 0)))
    columns = jnp.concatenate(
        [spaced[:, :, kh : kh + height, kw : kw + width, :] for kh in range(3) for kw in range(3)], axis=-1
    )
    columns = columns.reshape(columns.shape[:2] + (height * width, 9 * chans))
    flat_grad = cotangent.reshape(-1, chans)
    pieces = [
        lax.dot_general(
            columns[:, kt : kt + frames].reshape(-1, 9 * chans),
            flat_grad,
            (((0,), (0,)), ((), ())),
            preferred_element_type=jnp.float32,
        )
        for kt in range(3)
    ]
    return jnp.stack(pieces).reshape(27, chans, chans)


def shards(clips, kernel, cotangent):
    wide = clips.astype(jnp.float32)
    act = jax.nn.silu(wide).astype(jnp.bfloat16)
    earlier = passed_along(act, "tm", 1)
    earlier, sent_cot = lax.optimization_barrier((earlier, cotangent))
    following = passed_along(sent_cot, "tm", -1)
    extended = jnp.concatenate([earlier, act], axis=1)

    terms = kernel_terms(extended, cotangent)
    terms = terms.reshape((3, 3, 3) + terms.shape[1:])
    grad_kernel = lax.psum_scatter(terms, ("tm", "dp"), scatter_dimension=3, tiled=True)

    conv = convolve(extended, kernel, False)
    output = (wide + conv).astype(jnp.bfloat16)
    cot_ext = jnp.concatenate([cotangent, following], axis=1)
    grad_act = convolve(cot_ext, kernel, True)
    sig = jax.nn.sigmoid(wide)
    grad_input = (
        cotangent.astype(jnp.float32) + grad_act * sig * (1.0 + wide * (1.0 - sig))
    ).astype(jnp.bfloat16)
    return (output, grad_input, grad_kernel)


def solution(mesh):
    in_specs = (
        P(("groups", "dp"), "tm", None, None, None),
        P(),
        P(("groups", "dp"), "tm", None, None, None),
    )
    out_specs = (
        P(("groups", "dp"), "tm", None, None, None),
        P(("groups", "dp"), "tm", None, None, None),
        P("groups", None, None, ("tm", "dp"), None),
    )
    return jax.shard_map(shards, mesh=mesh, in_specs=in_specs, out_specs=out_specs, check_vma=False)
```

time: 167 us -> 197 us (1.18)
  local copies, waits for them, and re-layouts: 35.9 us -> 64.6 us
  waiting for transfers between devices: 75.8 us -> 79 us
  matrix products: 27.8 us -> 24.9 us
    transpose x1 -> x0, matrix products: 15.3 us -> none  [kernel_terms(): return jnp.transpose(terms, (1, 2, 3, 0, 4))]
    concatenate x0 -> x2, local copies, waits for them, and re-layouts: none -> 14.1 us  [kernel_terms(): jnp.concatenate([spaced[:, :, kh:kh + height, kw:kw + width, :] for kh in...]
    dot_general x0 -> x3, matrix products: none -> 12.4 us  [kernel_terms(): lax.dot_general(columns[:, kt:kt + frames].reshape(-1, 9 * chans), flat_g...]
    slice x0 -> x1, local copies, waits for them, and re-layouts: none -> 10.9 us  [kernel_terms(): columns[:, kt:kt + frames].reshape(-1, 9 * chans)]
    reshape x3, local copies, waits for them, and re-layouts: 9.2 us -> 19.9 us  [kernel_terms(): columns[:, kt:kt + frames].reshape(-1, 9 * chans)]
    reduce_scatter x1, waiting for transfers between devices: 54 us -> 63.1 us  [shards(): lax.psum_scatter(terms, ('tm', 'dp'), scatter_dimension=3, tiled=True)]
    unnamed x16 -> x26, local copies, waits for them, and re-layouts: 7.29 us -> 13.6 us
    ppermute x2, waiting for transfers between devices: 21.8 us -> 15.9 us  [passed_along(): lax.ppermute(value, axis, [(source, source + steps) for source in range(l...]
  transfers between devices with their start and end apart: 5 -> 3, of which waited for: 3 -> 3; matrix products, arithmetic and copies ran while one was open for 28% -> 12% of each run, Pallas kernels for 0% -> 0%
where the time goes in v2:
time: 197 us
  waiting for transfers between devices  79 us (40%)
  local copies, waits for them, and re-layouts  64.6 us (33%)
  matrix products  24.9 us (13%)
  between operations  14.2 us (7%)
  other arithmetic  7.52 us (4%)
  starting transfers between devices  6.48 us (3%)
    reduce_scatter x1, waiting for transfers between devices, shards(): lax.psum_scatter(terms, ('tm', 'dp'), scatter_dimension=3, tiled=True)  63.1 us
    reshape x3, local copies, waits for them, and re-layouts, kernel_terms(): columns[:, kt:kt + frames].reshape(-1, 9 * chans)  19.9 us
    ppermute x2, waiting for transfers between devices, passed_along(): lax.ppermute(value, axis, [(source, source + steps) for source in range(l...  15.9 us
    concatenate x2, local copies, waits for them, and re-layouts, kernel_terms(): jnp.concatenate([spaced[:, :, kh:kh + height, kw:kw + width, :] for kh in...  14.1 us
    unnamed x26, local copies, waits for them, and re-layouts  13.6 us
    conv_general_dilated x2, matrix products, convolve(): lax.conv_general_dilated(source, kernel, (1, 1, 1), [(0, 0), (1, 1), (1,...  12.6 us
    dot_general x3, matrix products, kernel_terms(): lax.dot_general(columns[:, kt:kt + frames].reshape(-1, 9 * chans), flat_g...  12.4 us
    slice x1, local copies, waits for them, and re-layouts, kernel_terms(): columns[:, kt:kt + frames].reshape(-1, 9 * chans)  10.9 us
  transfers between devices with their start and end apart: 3, of which 3 were waited for; matrix products, arithmetic and copies ran while one was open for 12% of the time, Pallas kernels for 0%

profile of v2, /device:TPU:0, one launch (start us, length us, event | category | flops | bytes accessed | tf_op | source)
XLA Modules:
  0.0 196.8 jit_solution(14500751751164523220)
XLA Ops:
  7.2 0.0 copy-start
  7.2 0.0 reduce-scatter.2.cloned.1.call-start
  7.2 1.5 fusion.35
  8.8 4.9 %collective-permute-start = (bf16[1,2,32,16,256]{4,2,3,1,0:T(8,128)(2,1)S(1)}, bf16[1,2,32,16,256]{4,2,3,1,0:T(8,128)(2,1)S(1)}, u32[]{:S(2)}, u32[]{:S(2)}) collective-permute-start(bf16[1,2,32,16,256]{4,2,3,1,0:T(8,128)(2,1)S(1)} %fusion.35), channel_id=1, source_target_pairs={{0,2},{2,4},{4,6},{6,8},{8,10},{10,12},{12,14},{1,3},{3,5},{5,7},{... | collective-permute-start | bytes 1572872 | tf_op jit(solution)/shard_map/ppermute | solution.py:10
  13.7 11.1 %collective-permute-done = bf16[1,2,32,16,256]{4,2,3,1,0:T(8,128)(2,1)S(1)} collective-permute-done((bf16[1,2,32,16,256]{4,2,3,1,0:T(8,128)(2,1)S(1)}, bf16[1,2,32,16,256]{4,2,3,1,0:T(8,128)(2,1)S(1)}, u32[]{:S(2)}, u32[]{:S(2)}) %collective-permute-start) | collective-permute-done | bytes 524320 | tf_op jit(solution)/shard_map/ppermute | solution.py:10
  24.8 0.1 pad_maximum_fusion.1
  24.9 1.4 fusion.24
  26.3 1.7 fusion.25
  28.1 1.6 fusion.26
  29.6 1.1 fusion.27
  30.7 1.8 constant_dynamic-update-slice_fusion
  32.5 1.2 fusion.28
  33.7 1.6 fusion.29
  35.2 1.7 fusion.30
  36.9 1.6 fusion.31
  38.5 12.5 %copy.31 = bf16[1,4,32,16,2304]{4,3,2,1,0:T(8,128)(2,1)} copy(bf16[1,4,32,16,2304]{4,2,3,1,0:T(8,128)(2,1)} %fusion.31) | data formatting | bytes 18874368 | tf_op jit(solution)/shard_map/concatenate | solution.py:32
  51.0 10.9 %fusion.49 = (bf16[1,2,512,2304]{3,2,1,0:T(8,128)(2,1)}, bf16[1,2,512,2304]{3,2,1,0:T(8,128)(2,1)}, bf16[1,2,512,2304]{3,2,1,0:T(8,128)(2,1)}) fusion(bf16[1,4,512,2304]{3,2,1,0:T(8,128)(2,1)} %bitcast.60), kind=kLoop, calls=%fused_computation.65 | loop fusion | bytes 28311552 | tf_op jit(solution)/shard_map/slice | solution.py:39
  61.9 6.6 %copy.32 = bf16[1024,2304]{0,1:T(8,128)(2,1)} copy(bf16[1024,2304]{1,0:T(8,128)(2,1)} %bitcast.63) | data formatting | bytes 9437184 | tf_op jit(solution)/shard_map/reshape | solution.py:39
  68.5 6.7 %copy.34 = bf16[1024,2304]{0,1:T(8,128)(2,1)} copy(bf16[1024,2304]{1,0:T(8,128)(2,1)} %bitcast.62) | data formatting | bytes 9437184 | tf_op jit(solution)/shard_map/reshape | solution.py:39
  75.3 0.0 copy-start.1
  75.3 0.0 copy-start.2
  75.3 5.4 %convolution_bitcast_fusion.2 = f32[1,3,3,256,256]{4,3,2,1,0:T(8,128)} fusion(bf16[3,3,256,1024]{3,2,1,0:T(8,128)(2,1)} %bitcast.66, bf16[1024,256,1,1]{1,0,3,2:T(8,128)(2,1)} %bitcast.69), kind=kOutput, calls=%fused_computation.30 | convolution fusion | flops 1207959552 | bytes 7602176 | tf_op jit(solution)/shard_map/dot_general | solution.py:38
  80.7 0.0 copy-done.1
  80.7 0.0 copy-done.2
  80.7 2.9 %convolution_bitcast_fusion = f32[1,3,3,256,256]{4,3,2,1,0:T(8,128)} fusion(bf16[3,3,256,1024]{3,2,1,0:T(8,128)(2,1)S(1)} %bitcast.67, bf16[1024,256,1,1]{1,0,3,2:T(8,128)(2,1)S(1)} %bitcast.71), kind=kOutput, calls=%fused_computation.28 | convolution fusion | flops 1207959552 | bytes 7602176 | tf_op jit(solution)/shard_map/dot_general | solution.py:38
  83.5 6.6 %copy.33 = bf16[1024,2304]{0,1:T(8,128)(2,1)} copy(bf16[1024,2304]{1,0:T(8,128)(2,1)} %bitcast.61) | data formatting | bytes 9437184 | tf_op jit(solution)/shard_map/reshape | solution.py:39
  90.1 0.0 copy-start.4
  90.1 0.0 copy-start.5
  90.1 4.1 %convolution_bitcast_fusion.1 = f32[1,3,3,256,256]{4,3,2,1,0:T(8,128)S(1)} fusion(bf16[3,3,256,1024]{3,2,1,0:T(8,128)(2,1)} %bitcast.68, bf16[1024,256,1,1]{1,0,3,2:T(8,128)(2,1)} %bitcast.70), kind=kOutput, calls=%fused_computation.29 | convolution fusion | flops 1207959552 | bytes 7602176 | tf_op jit(solution)/shard_map/dot_general | solution.py:38
  94.2 0.0 copy-done.4
  94.2 0.0 copy-done.5
  94.2 3.4 %pad_maximum_fusion = f32[3,3,3,256,256]{4,3,2,1,0:T(8,128)} fusion(f32[1,3,3,256,256]{4,3,2,1,0:T(8,128)S(1)} %copy-done.5, f32[1,3,3,256,256]{4,3,2,1,0:T(8,128)S(1)} %convolution_bitcast_fusion.1, f32[1,3,3,256,256]{4,3,2,1,0:T(8,128)S(1)} %copy-done.4), kind=kLoop, calls=%fused_computation | loop fusion | flops 3538944 | bytes 14155776 | tf_op jit(solution)/shard_map/stack | solution.py:46
  97.6 0.0 reduce-scatter.2.cloned.1.call-update
  97.6 1.2 copy.25
  98.8 0.0 copy-start.7
  98.8 1.2 copy.26
  100.1 1.5 collective-permute-start.1
  101.6 1.4 pad.5
  103.0 0.9 copy.23
  103.9 0.2 slice.49
  104.1 0.0 copy-done
  104.2 0.0 copy-done.7
  104.2 6.1 %fusion.19 = f32[2,32,8,3,256]{4,2,3,1,0:T(8,128)S(1)} fusion(bf16[3,3,3,256,256]{4,3,2,1,0:T(8,128)(2,1)S(1)} %copy-done, bf16[4,32,1,7,2,256]{5,3,4,1,0,2:T(8,128)(2,1)S(1)} %slice.49, bf16[4,32,1,8,3,256]{5,3,4,1,0,2:T(8,128)(2,1)S(1)} %copy.23, pred[8,3]{0,1:T(4,128)(4,1)S(1)} %copy-done.7), kind=kOutput, calls=%fused_computation.32 | convolution fusion | flops 5330829312 | bytes 7602200 | tf_op jit(solution)/shard_map/conv_general_dilated | solution.py:19
  110.3 0.5 copy.24
  110.8 4.7 %collective-permute-done.1 = bf16[1,2,32,16,256]{4,2,3,1,0:T(8,128)(2,1)S(1)} collective-permute-done((bf16[1,2,32,16,256]{4,2,3,1,0:T(8,128)(2,1)S(1)}, bf16[1,2,32,16,256]{4,2,3,1,0:T(8,128)(2,1)S(1)}, u32[]{:S(2)}, u32[]{:S(2)}) %collective-permute-start.1) | collective-permute-done | bytes 524320 | tf_op jit(solution)/shard_map/ppermute | solution.py:10
  115.5 0.1 maximum_bitcast_fusion
  115.6 0.2 pad.7
  115.8 0.9 copy.29
  116.7 0.2 slice.51
  117.0 0.0 copy-start.3
  117.0 0.0 copy-start.6
  117.0 6.4 %fusion.16 = f32[2,32,8,3,256]{4,2,3,1,0:T(8,128)S(1)} fusion(bf16[3,3,3,256,256]{4,3,2,1,0:T(8,128)(2,1)S(1)} %copy-done, bf16[4,32,1,7,2,256]{5,3,4,1,0,2:T(8,128)(2,1)S(1)} %slice.51, bf16[4,32,1,8,3,256]{5,3,4,1,0,2:T(8,128)(2,1)S(1)} %copy.29, pred[8,3]{0,1:T(4,128)(4,1)S(1)} %copy-done.7), kind=kOutput, calls=%fused_computation.31 | convolution fusion | flops 5330829312 | bytes 7602200 | tf_op jit(solution)/shard_map/conv_general_dilated | solution.py:19
  123.4 0.5 copy.30
  123.9 0.0 copy-done.3
  123.9 0.0 copy-done.6
  123.9 0.7 fusion.40
  124.6 1.1 copy.36
  125.7 1.1 copy.35
  126.8 63.1 %reduce-scatter.2.cloned.1.call-done = f32[3,3,3,16,256]{4,3,2,1,0:T(8,128)} async-done(((f32[3,3,3,256,256]{4,3,2,1,0:T(8,128)}), f32[3,3,3,16,256]{4,3,2,1,0:T(8,128)}) %reduce-scatter.2.cloned.1.call-update) | async-done | bytes 442384 | tf_op jit(solution)/shard_map/reduce_scatter | solution.py:59
Async XLA Ops:
  7.2 97.0 %copy-start = (bf16[3,3,3,256,256]{4,3,2,1,0:T(8,128)(2,1)S(1)}, bf16[3,3,3,256,256]{4,3,2,1,0:T(8,128)(2,1)}, u32[]{:S(2)}) copy-start(bf16[3,3,3,256,256]{4,3,2,1,0:T(8,128)(2,1)} %param.4) | copy-start | bytes 10616836
  7.2 182.7 %reduce-scatter.2.cloned.1.call-start = ((), (), s32[]{:S(2)}) async-start(), calls=%async_computation.1 | async-start | bytes 7520256 | tf_op jit(solution)/shard_map/reduce_scatter | solution.py:59
  8.8 16.1 %collective-permute-start = (bf16[1,2,32,16,256]{4,2,3,1,0:T(8,128)(2,1)S(1)}, bf16[1,2,32,16,256]{4,2,3,1,0:T(8,128)(2,1)S(1)}, u32[]{:S(2)}, u32[]{:S(2)}) collective-permute-start(bf16[1,2,32,16,256]{4,2,3,1,0:T(8,128)(2,1)S(1)} %fusion.35), channel_id=1, source_target_pairs={{0,2},{2,4},{4,6},{6,8},{8,10},{10,12},{12,14},{1,3},{3,5},{5,7},{... | collective-permute-start | bytes 1572872 | tf_op jit(solution)/shard_map/ppermute | solution.py:10
  75.3 5.4 %copy-start.1 = (bf16[1024,2304]{0,1:T(8,128)(2,1)S(1)}, bf16[1024,2304]{0,1:T(8,128)(2,1)}, u32[]{:S(2)}) copy-start(bf16[1024,2304]{0,1:T(8,128)(2,1)} %copy.34) | copy-start | bytes 14155780
  75.3 5.4 %copy-start.2 = (bf16[1,2,32,16,256]{4,3,2,1,0:T(8,128)(2,1)S(1)}, bf16[1,2,32,16,256]{4,3,2,1,0:T(8,128)(2,1)}, u32[]{:S(2)}) copy-start(bf16[1,2,32,16,256]{4,3,2,1,0:T(8,128)(2,1)} %param.5) | copy-start | bytes 1572868
  90.1 4.1 %copy-start.4 = (f32[1,3,3,256,256]{4,3,2,1,0:T(8,128)S(1)}, f32[1,3,3,256,256]{4,3,2,1,0:T(8,128)}, u32[]{:S(2)}) copy-start(f32[1,3,3,256,256]{4,3,2,1,0:T(8,128)} %convolution_bitcast_fusion.2) | copy-start | bytes 7077892
  90.1 4.1 %copy-start.5 = (f32[1,3,3,256,256]{4,3,2,1,0:T(8,128)S(1)}, f32[1,3,3,256,256]{4,3,2,1,0:T(8,128)}, u32[]{:S(2)}) copy-start(f32[1,3,3,256,256]{4,3,2,1,0:T(8,128)} %convolution_bitcast_fusion) | copy-start | bytes 7077892
  98.8 5.3 %copy-start.7 = (pred[8,3]{0,1:T(4,128)(4,1)S(1)}, pred[8,3]{0,1:T(4,128)(4,1)}, u32[]{:S(2)}) copy-start(pred[8,3]{0,1:T(4,128)(4,1)} %constant.19) | copy-start | bytes 76
  100.1 15.5 %collective-permute-start.1 = (bf16[1,2,32,16,256]{4,2,3,1,0:T(8,128)(2,1)S(1)}, bf16[1,2,32,16,256]{4,2,3,1,0:T(8,128)(2,1)S(1)}, u32[]{:S(2)}, u32[]{:S(2)}) collective-permute-start(bf16[1,2,32,16,256]{4,2,3,1,0:T(8,128)(2,1)S(1)} %copy.26), channel_id=1, source_target_pairs={{2,0},{4,2},{6,4},{8,6},{10,8},{12,10},{14,12},{3,1},{5,3},{7,5},{... | collective-permute-start | bytes 1572872 | tf_op jit(solution)/shard_map/ppermute | solution.py:10
  117.0 6.9 %copy-start.3 = (bf16[1,2,32,16,256]{4,3,2,1,0:T(8,128)(2,1)S(1)}, bf16[1,2,32,16,256]{4,3,2,1,0:T(8,128)(2,1)}, u32[]{:S(2)}) copy-start(bf16[1,2,32,16,256]{4,3,2,1,0:T(8,128)(2,1)} %param.5) | copy-start | bytes 1572868
  117.0 6.9 %copy-start.6 = (bf16[1,2,32,16,256]{4,3,2,1,0:T(8,128)(2,1)S(1)}, bf16[1,2,32,16,256]{4,3,2,1,0:T(8,128)(2,1)}, u32[]{:S(2)}) copy-start(bf16[1,2,32,16,256]{4,3,2,1,0:T(8,128)(2,1)} %param.3) | copy-start | bytes 1572868
Sparse Core Ops, SparseCore 0:
  97.7 92.1 reduce-scatter.1

commit v3 on v2

--- a/solution.py
+++ b/solution.py
@@ -10,7 +10,7 @@
     return lax.ppermute(value, axis, [(source, source + steps) for source in range(leading, last)])
 
 
-def convolve(source, kernel, flipped):
+def convolve(source, kernel, time_pad, flipped):
     if flipped:
         kernel = lax.rev(kernel, (0, 1, 2))
         layout = "DHWOI"
@@ -20,7 +20,7 @@
         source,
         kernel,
         (1, 1, 1),
-        [(0, 0), (1, 1), (1, 1)],
+        [time_pad, (1, 1), (1, 1)],
         dimension_numbers=("NDHWC", layout, "NDHWC"),
         preferred_element_type=jnp.float32,
     )
@@ -36,36 +36,35 @@
     flat_grad = cotangent.reshape(-1, chans)
     pieces = [
         lax.dot_general(
+            flat_grad,
             columns[:, kt : kt + frames].reshape(-1, 9 * chans),
-            flat_grad,
             (((0,), (0,)), ((), ())),
             preferred_element_type=jnp.float32,
         )
         for kt in range(3)
     ]
-    return jnp.stack(pieces).reshape(27, chans, chans)
+    return jnp.transpose(jnp.stack(pieces).reshape(3, chans, 9, chans), (0, 2, 3, 1)).reshape(27, chans, chans)
 
 
 def shards(clips, kernel, cotangent):
+    frames = clips.shape[1]
     wide = clips.astype(jnp.float32)
     act = jax.nn.silu(wide).astype(jnp.bfloat16)
     earlier = passed_along(act, "tm", 1)
-    earlier, sent_cot = lax.optimization_barrier((earlier, cotangent))
-    following = passed_along(sent_cot, "tm", -1)
     extended = jnp.concatenate([earlier, act], axis=1)
-
-    terms = kernel_terms(extended, cotangent)
-    terms = terms.reshape((3, 3, 3) + terms.shape[1:])
-    grad_kernel = lax.psum_scatter(terms, ("tm", "dp"), scatter_dimension=3, tiled=True)
-
-    conv = convolve(extended, kernel, False)
+    conv = convolve(extended, kernel, (0, 0), False)
     output = (wide + conv).astype(jnp.bfloat16)
-    cot_ext = jnp.concatenate([cotangent, following], axis=1)
-    grad_act = convolve(cot_ext, kernel, True)
+    padded_grad = jnp.pad(cotangent, ((0, 0), (2, 2), (0, 0), (0, 0), (0, 0)))
+    partial_grad = convolve(padded_grad, kernel, (0, 0), True)
+    returned = passed_along(partial_grad[:, :2].astype(jnp.bfloat16), "tm", -1).astype(jnp.float32)
+    returned = jnp.pad(returned, ((0, 0), (0, frames - 2), (0, 0), (0, 0), (0, 0)))
+    grad_act = partial_grad[:, 2:] + returned
     sig = jax.nn.sigmoid(wide)
     grad_input = (
         cotangent.astype(jnp.float32) + grad_act * sig * (1.0 + wide * (1.0 - sig))
     ).astype(jnp.bfloat16)
+    terms = kernel_terms(extended, cotangent).reshape((3, 3, 3) + (cotangent.shape[-1],) * 2)
+    grad_kernel = lax.psum_scatter(terms, ("tm", "dp"), scatter_dimension=3, tiled=True)
     return (output, grad_input, grad_kernel)
 
 

time: 197 us -> 176 us (0.89); the launches traced: 197 us -> 174 us
  local copies, waits for them, and re-layouts: 64.6 us -> 37.1 us
  matrix products: 24.9 us -> 34.6 us
  waiting for transfers between devices: 79 us -> 73.5 us
    reshape x3 -> x0, local copies, waits for them, and re-layouts: 19.9 us -> none  [kernel_terms(): columns[:, kt:kt + frames].reshape(-1, 9 * chans)]
    conv_general_dilated x2, matrix products: 12.6 us -> 30.1 us  [convolve(): lax.conv_general_dilated(source, kernel, (1, 1, 1), [time_pad, (1, 1), (1...]
    reduce_scatter x1, waiting for transfers between devices: 63.1 us -> 48.3 us  [shards(): lax.psum_scatter(terms, ('tm', 'dp'), scatter_dimension=3, tiled=True)]
    ppermute x2, waiting for transfers between devices: 15.9 us -> 25.2 us  [passed_along(): lax.ppermute(value, axis, [(source, source + steps) for source in range(l...]
    dot_general x3, matrix products: 12.4 us -> 4.46 us  [kernel_terms(): lax.dot_general(flat_grad, columns[:, kt:kt + frames].reshape(-1, 9 * cha...]
    slice x1, local copies, waits for them, and re-layouts: 10.9 us -> 6.03 us  [kernel_terms(): columns[:, kt:kt + frames].reshape(-1, 9 * chans)]
    unnamed x26 -> x23, local copies, waits for them, and re-layouts: 13.6 us -> 13.7 us
  transfers between devices with their start and end apart: 3 -> 3, of which waited for: 3 -> 3; matrix products, arithmetic and copies ran while one was open for 12% -> 22% of each run, Pallas kernels for 0% -> 0%
where the time goes in v3:
time: 176 us; the launch traced here: 174 us
  waiting for transfers between devices  73.5 us (42%)
  local copies, waits for them, and re-layouts  37.1 us (21%)
  matrix products  34.6 us (20%)
  between operations  14.4 us (8%)
  other arithmetic  7.55 us (4%)
  starting transfers between devices  6.39 us (4%)
    reduce_scatter x1, waiting for transfers between devices, shards(): lax.psum_scatter(terms, ('tm', 'dp'), scatter_dimension=3, tiled=True)  48.3 us
    conv_general_dilated x2, matrix products, convolve(): lax.conv_general_dilated(source, kernel, (1, 1, 1), [time_pad, (1, 1), (1...  30.1 us
    ppermute x2, waiting for transfers between devices, passed_along(): lax.ppermute(value, axis, [(source, source + steps) for source in range(l...  25.2 us
    concatenate x2, local copies, waits for them, and re-layouts, kernel_terms(): jnp.concatenate([spaced[:, :, kh:kh + height, kw:kw + width, :] for kh in...  14.1 us
    unnamed x23, local copies, waits for them, and re-layouts  13.7 us
    ppermute x2, starting transfers between devices, passed_along(): lax.ppermute(value, axis, [(source, source + steps) for source in range(l...  6.36 us
    slice x1, local copies, waits for them, and re-layouts, kernel_terms(): columns[:, kt:kt + frames].reshape(-1, 9 * chans)  6.03 us
    dot_general x3, matrix products, kernel_terms(): lax.dot_general(flat_grad, columns[:, kt:kt + frames].reshape(-1, 9 * cha...  4.46 us
  transfers between devices with their start and end apart: 3, of which 3 were waited for; matrix products, arithmetic and copies ran while one was open for 22% of the time, Pallas kernels for 0%

profile of v3, /device:TPU:0, one launch (start us, length us, event | category | flops | bytes accessed | tf_op | source)
XLA Modules:
  0.0 173.6 jit_solution(12852754943832081408)
XLA Ops:
  7.2 0.0 copy-start
  7.2 0.0 reduce-scatter.2.cloned.1.call-start
  7.2 1.5 fusion.30
  8.8 4.9 %collective-permute-start = (bf16[1,2,32,16,256]{4,2,3,1,0:T(8,128)(2,1)S(1)}, bf16[1,2,32,16,256]{4,2,3,1,0:T(8,128)(2,1)S(1)}, u32[]{:S(2)}, u32[]{:S(2)}) collective-permute-start(bf16[1,2,32,16,256]{4,2,3,1,0:T(8,128)(2,1)S(1)} %fusion.30), channel_id=1, source_target_pairs={{0,2},{2,4},{4,6},{6,8},{8,10},{10,12},{12,14},{1,3},{3,5},{5,7},{... | collective-permute-start | bytes 1572872 | tf_op jit(solution)/shard_map/ppermute | solution.py:10
  13.7 11.1 %collective-permute-done = bf16[1,2,32,16,256]{4,2,3,1,0:T(8,128)(2,1)S(1)} collective-permute-done((bf16[1,2,32,16,256]{4,2,3,1,0:T(8,128)(2,1)S(1)}, bf16[1,2,32,16,256]{4,2,3,1,0:T(8,128)(2,1)S(1)}, u32[]{:S(2)}, u32[]{:S(2)}) %collective-permute-start) | collective-permute-done | bytes 524320 | tf_op jit(solution)/shard_map/ppermute | solution.py:10
  24.8 0.1 pad_maximum_fusion.1
  24.9 1.4 fusion.19
  26.3 1.6 fusion.20
  27.9 1.5 fusion.21
  29.4 1.2 fusion.22
  30.7 1.7 constant_dynamic-update-slice_fusion
  32.4 1.2 fusion.23
  33.6 1.6 fusion.24
  35.2 1.7 fusion.25
  36.8 1.6 fusion.26
  38.4 12.6 %copy.28 = bf16[1,4,32,16,2304]{4,3,2,1,0:T(8,128)(2,1)} copy(bf16[1,4,32,16,2304]{4,2,3,1,0:T(8,128)(2,1)} %fusion.26) | data formatting | bytes 18874368 | tf_op jit(solution)/shard_map/concatenate | solution.py:32
  51.0 0.0 copy-start.2
  51.0 6.0 %fusion.46 = (bf16[1,2,512,2304]{3,2,1,0:T(8,128)(2,1)S(1)}, bf16[1,2,512,2304]{3,2,1,0:T(8,128)(2,1)S(1)}, bf16[1,2,512,2304]{3,2,1,0:T(8,128)(2,1)S(1)}) fusion(bf16[1,4,512,2304]{3,2,1,0:T(8,128)(2,1)} %bitcast.57), kind=kLoop, calls=%fused_computation.65 | loop fusion | bytes 28311552 | tf_op jit(solution)/shard_map/slice | solution.py:40
  57.0 0.0 copy-done.2
  57.0 1.5 fusion.47
  58.5 1.5 fusion.49
  60.0 1.5 fusion.48
  61.5 3.4 %pad_maximum_fusion = f32[3,256,9,256]{1,3,2,0:T(8,128)} fusion(f32[1,256,9,256]{1,3,2,0:T(8,128)S(1)} %bitcast.67, f32[1,256,9,256]{1,3,2,0:T(8,128)S(1)} %bitcast.68, f32[1,256,9,256]{1,3,2,0:T(8,128)S(1)} %bitcast.66), kind=kLoop, calls=%fused_computation | loop fusion | flops 3538944 | bytes 14155776 | tf_op jit(solution)/shard_map/stack | solution.py:46
  64.9 0.0 reduce-scatter.2.cloned.1.call-update
  64.9 0.0 copy-start.5
  64.9 1.2 copy.36
  66.1 0.1 pad.9
  66.2 0.4 copy.25
  66.6 0.1 slice.63
  66.8 0.0 copy-done
  66.8 0.0 copy-done.5
  66.8 24.0 %convolution_select_fusion = f32[4,32,8,3,256]{4,2,3,1,0:T(8,128)S(1)} fusion(bf16[3,3,3,256,256]{4,3,2,1,0:T(8,128)(2,1)S(1)} %copy-done, pred[8,3]{0,1:T(4,128)(4,1)S(1)} %copy-done.5, bf16[2,32,1,7,2,256]{5,3,4,1,0,2:T(8,128)(2,1)S(1)} %slice.63, bf16[2,32,1,8,3,256]{5,3,4,1,0,2:T(8,128)(2,1)S(1)} %copy.25), kind=kOutput, calls=%fused_computation.11 | convolution fusion | flops 5327290368 | bytes 7929880 | tf_op jit(solution)/shard_map/conv_general_dilated | solution.py:19
  90.8 0.1 slice.107
  90.9 0.2 copy.27
  91.1 0.0 copy-start.1
  91.1 1.4 collective-permute-start.1
  92.6 0.1 slice.64
  92.7 0.5 copy.26
  93.2 0.0 copy-done.1
  93.2 0.2 pad.7
  93.4 0.9 copy.20
  94.3 0.2 slice.61
  94.5 0.0 copy-start.3
  94.5 0.0 copy-start.4
  94.5 6.1 %fusion.9 = f32[2,32,8,3,256]{4,2,3,1,0:T(8,128)S(1)} fusion(bf16[3,3,3,256,256]{4,3,2,1,0:T(8,128)(2,1)S(1)} %copy-done, bf16[4,32,1,7,2,256]{5,3,4,1,0,2:T(8,128)(2,1)S(1)} %slice.61, bf16[4,32,1,8,3,256]{5,3,4,1,0,2:T(8,128)(2,1)S(1)} %copy.20, pred[8,3]{0,1:T(4,128)(4,1)S(1)} %copy-done.5), kind=kOutput, calls=%fused_computation.25 | convolution fusion | flops 5330829312 | bytes 7602200 | tf_op jit(solution)/shard_map/conv_general_dilated | solution.py:19
  100.7 0.5 copy.21
  101.2 14.1 %collective-permute-done.1 = bf16[1,2,32,16,256]{4,2,3,1,0:T(8,128)(2,1)S(1)} collective-permute-done((bf16[1,2,32,16,256]{4,2,3,1,0:T(8,128)(2,1)S(1)}, bf16[1,2,32,16,256]{4,2,3,1,0:T(8,128)(2,1)S(1)}, u32[]{:S(2)}, u32[]{:S(2)}) %collective-permute-start.1) | collective-permute-done | bytes 524320 | tf_op jit(solution)/shard_map/ppermute | solution.py:10
  115.2 0.0 copy-done.3
  115.2 0.0 copy-done.4
  115.2 0.8 fusion.35
  116.1 1.1 copy.30
  117.2 1.1 copy.29
  118.3 48.3 %reduce-scatter.2.cloned.1.call-done = f32[3,3,3,16,256]{4,3,2,1,0:T(8,128)} async-done(((f32[3,3,3,256,256]{4,3,2,1,0:T(8,128)}), f32[3,3,3,16,256]{4,3,2,1,0:T(8,128)}) %reduce-scatter.2.cloned.1.call-update) | async-done | bytes 442384 | tf_op jit(solution)/shard_map/reduce_scatter | solution.py:67
  (1 shorter events, 0.0 us)
Async XLA Ops:
  7.2 59.6 %copy-start = (bf16[3,3,3,256,256]{4,3,2,1,0:T(8,128)(2,1)S(1)}, bf16[3,3,3,256,256]{4,3,2,1,0:T(8,128)(2,1)}, u32[]{:S(2)}) copy-start(bf16[3,3,3,256,256]{4,3,2,1,0:T(8,128)(2,1)} %param.4) | copy-start | bytes 10616836
  7.2 159.4 %reduce-scatter.2.cloned.1.call-start = ((), (), s32[]{:S(2)}) async-start(), calls=%async_computation.1 | async-start | bytes 7520256 | tf_op jit(solution)/shard_map/reduce_scatter | solution.py:67
  8.8 16.1 %collective-permute-start = (bf16[1,2,32,16,256]{4,2,3,1,0:T(8,128)(2,1)S(1)}, bf16[1,2,32,16,256]{4,2,3,1,0:T(8,128)(2,1)S(1)}, u32[]{:S(2)}, u32[]{:S(2)}) collective-permute-start(bf16[1,2,32,16,256]{4,2,3,1,0:T(8,128)(2,1)S(1)} %fusion.30), channel_id=1, source_target_pairs={{0,2},{2,4},{4,6},{6,8},{8,10},{10,12},{12,14},{1,3},{3,5},{5,7},{... | collective-permute-start | bytes 1572872 | tf_op jit(solution)/shard_map/ppermute | solution.py:10
  51.0 6.0 %copy-start.2 = (bf16[1,2,32,16,256]{4,3,2,1,0:T(8,128)(2,1)S(1)}, bf16[1,2,32,16,256]{4,3,2,1,0:T(8,128)(2,1)}, u32[]{:S(2)}) copy-start(bf16[1,2,32,16,256]{4,3,2,1,0:T(8,128)(2,1)} %param.5) | copy-start | bytes 1572868
  64.9 1.9 %copy-start.5 = (pred[8,3]{0,1:T(4,128)(4,1)S(1)}, pred[8,3]{0,1:T(4,128)(4,1)}, u32[]{:S(2)}) copy-start(pred[8,3]{0,1:T(4,128)(4,1)} %constant.19) | copy-start | bytes 76
  91.1 2.1 %copy-start.1 = (bf16[4,32,1,16,256]{4,1,3,0,2:T(8,128)(2,1)S(1)}, bf16[4,32,1,16,256]{4,1,3,0,2:T(8,128)(2,1)}, u32[]{:S(2)}) copy-start(bf16[4,32,1,16,256]{4,1,3,0,2:T(8,128)(2,1)} %get-tuple-element.13) | copy-start | bytes 3145732
  91.1 24.1 %collective-permute-start.1 = (bf16[1,2,32,16,256]{4,2,3,1,0:T(8,128)(2,1)S(1)}, bf16[1,2,32,16,256]{4,2,3,1,0:T(8,128)(2,1)S(1)}, u32[]{:S(2)}, u32[]{:S(2)}) collective-permute-start(bf16[1,2,32,16,256]{4,2,3,1,0:T(8,128)(2,1)S(1)} %slice_bitcast_fusion.2), channel_id=1, source_target_pairs={{2,0},{4,2},{6,4},{8,6},{10,8},{12,10},{14,12},{3,1},{5,3},{7,5},{... | collective-permute-start | bytes 1572872 | tf_op jit(solution)/shard_map/ppermute | solution.py:10
  94.5 20.7 %copy-start.3 = (bf16[1,2,32,16,256]{4,3,2,1,0:T(8,128)(2,1)S(1)}, bf16[1,2,32,16,256]{4,3,2,1,0:T(8,128)(2,1)}, u32[]{:S(2)}) copy-start(bf16[1,2,32,16,256]{4,3,2,1,0:T(8,128)(2,1)} %param.5) | copy-start | bytes 1572868
  94.5 20.7 %copy-start.4 = (bf16[1,2,32,16,256]{4,3,2,1,0:T(8,128)(2,1)S(1)}, bf16[1,2,32,16,256]{4,3,2,1,0:T(8,128)(2,1)}, u32[]{:S(2)}) copy-start(bf16[1,2,32,16,256]{4,3,2,1,0:T(8,128)(2,1)} %param.3) | copy-start | bytes 1572868
Sparse Core Ops, SparseCore 0:
  65.0 101.5 reduce-scatter.1

commit v4 on v0

--- a/solution.py
+++ b/solution.py
@@ -26,28 +26,30 @@
     )
 
 
-def kernel_terms(extended, cotangent):
+def kernel_terms(extended, own, cotangent):
     frames = cotangent.shape[1]
     height = cotangent.shape[2]
     width = cotangent.shape[3]
     chans = cotangent.shape[4]
     spaced = jnp.pad(extended, ((0, 0), (0, 0), (1, 1), (1, 1), (0, 0)))
+    spaced_own = jnp.pad(own, ((0, 0), (0, 0), (1, 1), (1, 1), (0, 0)))
     flat_grad = cotangent.reshape(-1, chans)
-    pieces = []
-    for kt in range(3):
+    pieces = {}
+    for kt in (2, 1, 0):
         for kh in range(3):
             for kw in range(3):
-                window = spaced[:, kt : kt + frames, kh : kh + height, kw : kw + width, :].reshape(
-                    -1, chans
+                if kt == 2:
+                    window = spaced_own[:, :, kh : kh + height, kw : kw + width, :]
+                else:
+                    window = spaced[:, kt : kt + frames, kh : kh + height, kw : kw + width, :]
+                window = window.reshape(-1, chans)
+                pieces[kt, kh, kw] = lax.dot_general(
+                    window,
+                    flat_grad,
+                    (((0,), (0,)), ((), ())),
+                    preferred_element_type=jnp.float32,
                 )
-                pieces.append(
-                    lax.dot_general(
-                        window,
-                        flat_grad,
-                        (((0,), (0,)), ((), ())),
-                        preferred_element_type=jnp.float32,
-                    )
-                )
+    pieces = [pieces[kt, kh, kw] for kt in (2, 1, 0) for kh in range(3) for kw in range(3)]
     return jnp.stack(pieces).reshape(3, 3, 3, chans, chans)
 
 
@@ -68,8 +70,8 @@
     grad_input = (
         cotangent.astype(jnp.float32) + grad_act * sig * (1.0 + wide * (1.0 - sig))
     ).astype(jnp.bfloat16)
-    terms = kernel_terms(extended, cotangent)
-    grad_kernel = lax.psum_scatter(terms, ("tm", "dp"), scatter_dimension=3, tiled=True)
+    terms = kernel_terms(extended, act, cotangent)
+    grad_kernel = lax.rev(lax.psum_scatter(terms, ("tm", "dp"), scatter_dimension=3, tiled=True), (0,))
     return (output, grad_input, grad_kernel)
 
 

time: 157 us -> 147 us (0.936)
  waiting for transfers between devices: 75 us -> 62.4 us
  local copies, waits for them, and re-layouts: 6.74 us -> 8.54 us
    ppermute x2, waiting for transfers between devices: 16.5 us -> 5.16 us  [passed_along(): lax.ppermute(value, axis, [(source, source + steps) for source in range(l...]
    rev x0 -> x1, local copies, waits for them, and re-layouts: none -> 1.8 us  [shards(): lax.rev(lax.psum_scatter(terms, ('tm', 'dp'), scatter_dimension=3, tiled=...]
  transfers between devices with their start and end apart: 3 -> 3, of which waited for: 3 -> 2; matrix products, arithmetic and copies ran while one was open for 17% -> 27% of each run, Pallas kernels for 0% -> 0%
where the time goes in v4:
time: 147 us
  waiting for transfers between devices  62.4 us (42%)
  matrix products  51.8 us (35%)
  between operations  14.2 us (10%)
  local copies, waits for them, and re-layouts  8.54 us (6%)
  starting transfers between devices  6.61 us (4%)
  other arithmetic  3.48 us (2%)
    reduce_scatter x1, waiting for transfers between devices, shards(): lax.psum_scatter(terms, ('tm', 'dp'), scatter_dimension=3, tiled=True)  57.3 us
    dot_general x27, matrix products, kernel_terms(): lax.dot_general(window, flat_grad, (((0,), (0,)), ((), ())), preferred_el...  32.7 us
    conv_general_dilated x2, matrix products, convolve(): lax.conv_general_dilated(source, kernel, (1, 1, 1), [time_pad, (1, 1), (1...  19.1 us
    ppermute x2, starting transfers between devices, passed_along(): lax.ppermute(value, axis, [(source, source + steps) for source in range(l...  6.58 us
    ppermute x2, waiting for transfers between devices, passed_along(): lax.ppermute(value, axis, [(source, source + steps) for source in range(l...  5.16 us
    unnamed x18, local copies, waits for them, and re-layouts  3.49 us
  transfers between devices with their start and end apart: 3, of which 2 were waited for; matrix products, arithmetic and copies ran while one was open for 27% of the time, Pallas kernels for 0%

profile of v4, /device:TPU:0, one launch (start us, length us, event | category | flops | bytes accessed | tf_op | source)
XLA Modules:
  0.0 147.1 jit_solution(5611813244503922492)
XLA Ops:
  7.2 0.0 copy-start
  7.2 0.0 reduce-scatter.2.cloned.1.call-start
  7.2 0.0 copy-start.2
  7.2 1.5 %fusion.49 = bf16[1,2,32,16,256]{4,2,3,1,0:T(8,128)(2,1)S(1)} fusion(bf16[1,2,32,16,256]{4,3,2,1,0:T(8,128)(2,1)} %param.3), kind=kLoop, calls=%fused_computation.99 | loop fusion | flops 1572864 | bytes 1048576 | tf_op jit(solution)/shard_map/convert_element_type | solution.py:59
  8.8 4.9 %collective-permute-start = (bf16[1,2,32,16,256]{4,2,3,1,0:T(8,128)(2,1)S(1)}, bf16[1,2,32,16,256]{4,2,3,1,0:T(8,128)(2,1)S(1)}, u32[]{:S(2)}, u32[]{:S(2)}) collective-permute-start(bf16[1,2,32,16,256]{4,2,3,1,0:T(8,128)(2,1)S(1)} %fusion.49), channel_id=1, source_target_pairs={{0,2},{2,4},{4,6},{6,8},{8,10},{10,12},{12,14},{1,3},{3,5},{5,7},{... | collective-permute-start | bytes 1572872 | tf_op jit(solution)/shard_map/ppermute | solution.py:10
  13.7 0.0 copy-start.4
  13.7 2.2 %fusion.45 = f32[27,256,256]{2,1,0:T(8,128)} fusion(bf16[1,2,32,16,256]{4,2,3,1,0:T(8,128)(2,1)S(1)} %fusion.49, bf16[2,32,16,256]{3,2,1,0:T(8,128)(2,1)} %bitcast.338), kind=kOutput, calls=%fused_computation.95 | convolution fusion | flops 134217728 | bytes 1310720 | tf_op jit(solution)/shard_map/dot_general | solution.py:46
  16.0 2.2 %fusion.44 = f32[27,256,256]{2,1,0:T(8,128)} fusion(f32[27,256,256]{2,1,0:T(8,128)} %fusion.45, bf16[1,2,32,16,256]{4,2,3,1,0:T(8,128)(2,1)S(1)} %fusion.49, bf16[2,32,16,256]{3,2,1,0:T(8,128)(2,1)} %bitcast.339), kind=kOutput, calls=%fused_computation.93 | convolution fusion | flops 134217728 | bytes 1310720 | tf_op jit(solution)/shard_map/dot_general | solution.py:46
  18.1 0.0 copy-done.2
  18.1 1.1 fusion.43
  19.3 1.1 fusion.42
  20.4 0.0 copy-done.4
  20.4 1.3 fusion.41
  21.7 1.1 fusion.40
  22.8 1.1 fusion.39
  23.9 1.1 fusion.38
  25.1 1.1 fusion.37
  26.2 0.0 collective-permute-done
  26.2 1.1 pad_maximum_fusion
  27.3 1.1 fusion.36
  28.4 1.1 fusion.35
  29.5 1.1 fusion.34
  30.7 1.1 fusion.33
  31.8 1.1 fusion.32
  32.9 1.1 fusion.31
  34.1 1.1 fusion.30
  35.2 1.1 fusion.29
  36.3 1.1 fusion.28
  37.4 1.1 fusion.27
  38.6 1.1 fusion.26
  39.7 1.1 fusion.25
  40.9 1.1 fusion.24
  42.0 1.1 fusion.23
  43.1 1.1 fusion.22
  44.2 1.1 fusion.21
  45.3 1.1 fusion.20
  46.4 1.1 fusion.19
  47.6 0.0 reduce-scatter.2.cloned.1.call-update
  47.6 1.2 copy.165
  48.8 0.1 pad.14
  48.9 0.4 copy.44
  49.3 0.1 slice.122
  49.5 0.0 copy-done
  49.5 12.9 %convolution_select_fusion = f32[4,32,8,3,256]{4,2,3,1,0:T(8,128)S(1)} fusion(bf16[3,3,3,256,256]{4,3,2,1,0:T(8,128)(2,1)S(1)} %copy-done, pred[8,3]{0,1:T(4,128)(4,1)S(1)} %copy-done.6, bf16[2,32,1,7,2,256]{5,3,4,1,0,2:T(8,128)(2,1)S(1)} %slice.122, bf16[2,32,1,8,3,256]{5,3,4,1,0,2:T(8,128)(2,1)S(1)} %copy.44), kind=kOutput, calls=%fused_computation.26 | convolution fusion | flops 5327290368 | bytes 7929880 | tf_op jit(solution)/shard_map/conv_general_dilated | solution.py:19
  62.4 0.1 slice.247
  62.5 0.2 copy.46
  62.7 1.6 %collective-permute-start.1 = (bf16[1,2,32,16,256]{4,2,3,1,0:T(8,128)(2,1)S(1)}, bf16[1,2,32,16,256]{4,2,3,1,0:T(8,128)(2,1)S(1)}, u32[]{:S(2)}, u32[]{:S(2)}) collective-permute-start(bf16[1,2,32,16,256]{4,2,3,1,0:T(8,128)(2,1)S(1)} %slice_bitcast_fusion.2), channel_id=1, source_target_pairs={{2,0},{4,2},{6,4},{8,6},{10,8},{12,10},{14,12},{3,1},{5,3},{7,5},{... | collective-permute-start | bytes 1572872 | tf_op jit(solution)/shard_map/ppermute | solution.py:10
  64.4 0.1 slice.123
  64.5 0.5 copy.45
  65.0 0.0 copy-done.1
  65.0 0.2 pad.12
  65.2 0.9 copy.39
  66.1 0.2 slice.120
  66.3 0.0 copy-start.3
  66.3 0.0 copy-start.5
  66.4 6.1 %fusion.9 = f32[2,32,8,3,256]{4,2,3,1,0:T(8,128)S(1)} fusion(bf16[3,3,3,256,256]{4,3,2,1,0:T(8,128)(2,1)S(1)} %copy-done, bf16[4,32,1,7,2,256]{5,3,4,1,0,2:T(8,128)(2,1)S(1)} %slice.120, bf16[4,32,1,8,3,256]{5,3,4,1,0,2:T(8,128)(2,1)S(1)} %copy.39, pred[8,3]{0,1:T(4,128)(4,1)S(1)} %copy-done.6), kind=kOutput, calls=%fused_computation.32 | convolution fusion | flops 5330829312 | bytes 7602200 | tf_op jit(solution)/shard_map/conv_general_dilated | solution.py:19
  72.5 0.5 copy.40
  73.0 5.2 %collective-permute-done.1 = bf16[1,2,32,16,256]{4,2,3,1,0:T(8,128)(2,1)S(1)} collective-permute-done((bf16[1,2,32,16,256]{4,2,3,1,0:T(8,128)(2,1)S(1)}, bf16[1,2,32,16,256]{4,2,3,1,0:T(8,128)(2,1)S(1)}, u32[]{:S(2)}, u32[]{:S(2)}) %collective-permute-start.1) | collective-permute-done | bytes 524320 | tf_op jit(solution)/shard_map/ppermute | solution.py:10
  78.1 0.0 copy-done.3
  78.1 0.8 fusion.54
  79.0 1.1 copy.75
  80.1 1.1 copy.74
  81.2 57.3 %reduce-scatter.2.cloned.1.call-done = f32[3,3,3,16,256]{4,3,2,1,0:T(8,128)} async-done(((f32[3,3,3,256,256]{4,3,2,1,0:T(8,128)}), f32[3,3,3,16,256]{4,3,2,1,0:T(8,128)}) %reduce-scatter.2.cloned.1.call-update) | async-done | bytes 442384 | tf_op jit(solution)/shard_map/reduce_scatter | solution.py:74
  138.4 1.8 %rev.4 = f32[3,3,3,16,256]{4,3,2,1,0:T(8,128)} reverse(f32[3,3,3,16,256]{4,3,2,1,0:T(8,128)} %reduce-scatter.2.cloned.1.call-done), dimensions={0} | reverse | bytes 884736 | tf_op jit(solution)/shard_map/rev | solution.py:74
  (5 shorter events, 0.0 us)
Async XLA Ops:
  7.2 42.3 %copy-start = (bf16[3,3,3,256,256]{4,3,2,1,0:T(8,128)(2,1)S(1)}, bf16[3,3,3,256,256]{4,3,2,1,0:T(8,128)(2,1)}, u32[]{:S(2)}) copy-start(bf16[3,3,3,256,256]{4,3,2,1,0:T(8,128)(2,1)} %param.4) | copy-start | bytes 10616836
  7.2 131.2 %reduce-scatter.2.cloned.1.call-start = ((), (), s32[]{:S(2)}) async-start(), calls=%async_computation.1 | async-start | bytes 7520256 | tf_op jit(solution)/shard_map/reduce_scatter | solution.py:74
  7.2 10.9 %copy-start.2 = (bf16[1,2,32,16,256]{4,3,2,1,0:T(8,128)(2,1)S(1)}, bf16[1,2,32,16,256]{4,3,2,1,0:T(8,128)(2,1)}, u32[]{:S(2)}) copy-start(bf16[1,2,32,16,256]{4,3,2,1,0:T(8,128)(2,1)} %param.5) | copy-start | bytes 1572868
  8.8 17.4 %collective-permute-start = (bf16[1,2,32,16,256]{4,2,3,1,0:T(8,128)(2,1)S(1)}, bf16[1,2,32,16,256]{4,2,3,1,0:T(8,128)(2,1)S(1)}, u32[]{:S(2)}, u32[]{:S(2)}) collective-permute-start(bf16[1,2,32,16,256]{4,2,3,1,0:T(8,128)(2,1)S(1)} %fusion.49), channel_id=1, source_target_pairs={{0,2},{2,4},{4,6},{6,8},{8,10},{10,12},{12,14},{1,3},{3,5},{5,7},{... | collective-permute-start | bytes 1572872 | tf_op jit(solution)/shard_map/ppermute | solution.py:10
  13.7 6.6 %copy-start.4 = (bf16[1,2,32,16,256]{4,3,2,1,0:T(8,128)(2,1)S(1)}, bf16[1,2,32,16,256]{4,3,2,1,0:T(8,128)(2,1)}, u32[]{:S(2)}) copy-start(bf16[1,2,32,16,256]{4,3,2,1,0:T(8,128)(2,1)} %param.3) | copy-start | bytes 1572868
  46.4 3.0 %copy-start.6 = (pred[8,3]{0,1:T(4,128)(4,1)S(1)}, pred[8,3]{0,1:T(4,128)(4,1)}, u32[]{:S(2)}) copy-start(pred[8,3]{0,1:T(4,128)(4,1)} %constant.21) | copy-start | bytes 76
  62.4 2.6 %copy-start.1 = (bf16[4,32,1,16,256]{4,1,3,0,2:T(8,128)(2,1)S(1)}, bf16[4,32,1,16,256]{4,1,3,0,2:T(8,128)(2,1)}, u32[]{:S(2)}) copy-start(bf16[4,32,1,16,256]{4,1,3,0,2:T(8,128)(2,1)} %get-tuple-element.10) | copy-start | bytes 3145732
  62.7 15.4 %collective-permute-start.1 = (bf16[1,2,32,16,256]{4,2,3,1,0:T(8,128)(2,1)S(1)}, bf16[1,2,32,16,256]{4,2,3,1,0:T(8,128)(2,1)S(1)}, u32[]{:S(2)}, u32[]{:S(2)}) collective-permute-start(bf16[1,2,32,16,256]{4,2,3,1,0:T(8,128)(2,1)S(1)} %slice_bitcast_fusion.2), channel_id=1, source_target_pairs={{2,0},{4,2},{6,4},{8,6},{10,8},{12,10},{14,12},{3,1},{5,3},{7,5},{... | collective-permute-start | bytes 1572872 | tf_op jit(solution)/shard_map/ppermute | solution.py:10
  66.3 11.8 %copy-start.3 = (bf16[1,2,32,16,256]{4,3,2,1,0:T(8,128)(2,1)S(1)}, bf16[1,2,32,16,256]{4,3,2,1,0:T(8,128)(2,1)}, u32[]{:S(2)}) copy-start(bf16[1,2,32,16,256]{4,3,2,1,0:T(8,128)(2,1)} %param.5) | copy-start | bytes 1572868
  66.3 11.8 %copy-start.5 = (bf16[1,2,32,16,256]{4,3,2,1,0:T(8,128)(2,1)S(1)}, bf16[1,2,32,16,256]{4,3,2,1,0:T(8,128)(2,1)}, u32[]{:S(2)}) copy-start(bf16[1,2,32,16,256]{4,3,2,1,0:T(8,128)(2,1)} %param.3) | copy-start | bytes 1572868
Sparse Core Ops, SparseCore 0:
  47.7 90.6 reduce-scatter.1

commit v5 on v4

--- a/solution.py
+++ b/solution.py
@@ -34,21 +34,25 @@
     spaced = jnp.pad(extended, ((0, 0), (0, 0), (1, 1), (1, 1), (0, 0)))
     spaced_own = jnp.pad(own, ((0, 0), (0, 0), (1, 1), (1, 1), (0, 0)))
     flat_grad = cotangent.reshape(-1, chans)
+    padded_grad = jnp.pad(cotangent, ((0, 0), (1, 1), (0, 0), (0, 0), (0, 0)))
+    shifted_grad = jnp.concatenate(
+        [padded_grad[:, 1 - kt : 2 - kt + frames] for kt in range(2)], axis=-1
+    ).reshape(-1, 2 * chans)
     pieces = {}
-    for kt in (2, 1, 0):
-        for kh in range(3):
-            for kw in range(3):
-                if kt == 2:
-                    window = spaced_own[:, :, kh : kh + height, kw : kw + width, :]
-                else:
-                    window = spaced[:, kt : kt + frames, kh : kh + height, kw : kw + width, :]
-                window = window.reshape(-1, chans)
-                pieces[kt, kh, kw] = lax.dot_general(
-                    window,
-                    flat_grad,
-                    (((0,), (0,)), ((), ())),
-                    preferred_element_type=jnp.float32,
-                )
+    for kh in range(3):
+        for kw in range(3):
+            window = spaced_own[:, :, kh : kh + height, kw : kw + width, :].reshape(-1, chans)
+            pieces[2, kh, kw] = lax.dot_general(
+                window, flat_grad, (((0,), (0,)), ((), ())), preferred_element_type=jnp.float32
+            )
+    for kh in range(3):
+        for kw in range(3):
+            window = spaced[:, : frames + 1, kh : kh + height, kw : kw + width, :].reshape(-1, chans)
+            both = lax.dot_general(
+                window, shifted_grad, (((0,), (0,)), ((), ())), preferred_element_type=jnp.float32
+            )
+            pieces[0, kh, kw] = both[:, :chans]
+            pieces[1, kh, kw] = both[:, chans:]
     pieces = [pieces[kt, kh, kw] for kt in (2, 1, 0) for kh in range(3) for kw in range(3)]
     return jnp.stack(pieces).reshape(3, 3, 3, chans, chans)
 

time: 147 us -> 146 us (level)
  matrix products: 51.8 us -> 36 us
  local copies, waits for them, and re-layouts: 8.54 us -> 22.8 us
    dot_general x27 -> x9, matrix products: 32.7 us -> 11.6 us  [kernel_terms(): lax.dot_general(window, flat_grad, (((0,), (0,)), ((), ())), preferred_el...]
    unnamed x18 -> x37, local copies, waits for them, and re-layouts: 3.49 us -> 16.8 us
    dot_general x0 -> x9, matrix products: none -> 5.41 us  [kernel_terms(): lax.dot_general(window, shifted_grad, (((0,), (0,)), ((), ())), preferred...]
where the time goes in v5:
time: 146 us; the launch traced here: 145 us
  waiting for transfers between devices  62.1 us (43%)
  matrix products  36 us (25%)
  local copies, waits for them, and re-layouts  22.8 us (16%)
  between operations  14.3 us (10%)
  starting transfers between devices  6.61 us (5%)
  other arithmetic  3.48 us (2%)
    reduce_scatter x1, waiting for transfers between devices, shards(): lax.psum_scatter(terms, ('tm', 'dp'), scatter_dimension=3, tiled=True)  57 us
    conv_general_dilated x2, matrix products, convolve(): lax.conv_general_dilated(source, kernel, (1, 1, 1), [time_pad, (1, 1), (1...  19.1 us
    unnamed x37, local copies, waits for them, and re-layouts  16.8 us
    dot_general x9, matrix products, kernel_terms(): lax.dot_general(window, flat_grad, (((0,), (0,)), ((), ())), preferred_el...  11.6 us
    ppermute x2, starting transfers between devices, passed_along(): lax.ppermute(value, axis, [(source, source + steps) for source in range(l...  6.58 us
    dot_general x9, matrix products, kernel_terms(): lax.dot_general(window, shifted_grad, (((0,), (0,)), ((), ())), preferred...  5.41 us
    ppermute x2, waiting for transfers between devices, passed_along(): lax.ppermute(value, axis, [(source, source + steps) for source in range(l...  5.16 us
  transfers between devices with their start and end apart: 3, of which 2 were waited for; matrix products, arithmetic and copies ran while one was open for 27% of the time, Pallas kernels for 0%

profile of v5, /device:TPU:0, one launch (start us, length us, event | category | flops | bytes accessed | tf_op | source)
XLA Modules:
  0.0 145.4 jit_solution(3063945881497053311)
XLA Ops:
  7.2 0.0 copy-start
  7.2 0.0 reduce-scatter.2.cloned.1.call-start
  7.2 1.5 %fusion.31 = bf16[1,2,32,16,256]{4,2,3,1,0:T(8,128)(2,1)S(1)} fusion(bf16[1,2,32,16,256]{4,3,2,1,0:T(8,128)(2,1)} %param.3), kind=kLoop, calls=%fused_computation.67 | loop fusion | flops 1572864 | bytes 1048576 | tf_op jit(solution)/shard_map/convert_element_type | solution.py:63
  8.8 4.9 %collective-permute-start = (bf16[1,2,32,16,256]{4,2,3,1,0:T(8,128)(2,1)S(1)}, bf16[1,2,32,16,256]{4,2,3,1,0:T(8,128)(2,1)S(1)}, u32[]{:S(2)}, u32[]{:S(2)}) collective-permute-start(bf16[1,2,32,16,256]{4,2,3,1,0:T(8,128)(2,1)S(1)} %fusion.31), channel_id=1, source_target_pairs={{0,2},{2,4},{4,6},{6,8},{8,10},{10,12},{12,14},{1,3},{3,5},{5,7},{... | collective-permute-start | bytes 1572872 | tf_op jit(solution)/shard_map/ppermute | solution.py:10
  13.7 1.2 copy.87
  14.9 2.4 %fusion.27 = f32[27,256,256]{2,1,0:T(8,128)} fusion(bf16[1,2,32,16,256]{4,2,3,1,0:T(8,128)(2,1)S(1)} %fusion.31, bf16[2,32,16,256]{3,2,1,0:T(8,128)(2,1)} %bitcast.286), kind=kOutput, calls=%fused_computation.63 | convolution fusion | flops 134217728 | bytes 1310720 | tf_op jit(solution)/shard_map/dot_general | solution.py:45
  17.3 1.1 fusion.26
  18.4 1.1 fusion.25
  19.6 1.1 fusion.24
  20.7 1.3 fusion.23
  22.0 1.1 fusion.22
  23.1 1.1 fusion.21
  24.2 0.2 pad_slice_fusion.11
  24.4 1.2 fusion.20
  25.6 1.1 fusion.19
  26.7 1.1 pad_maximum_fusion
  27.8 0.6 convolution_bitcast_fusion.6
  28.4 0.6 convolution_bitcast_fusion.5
  29.0 0.6 convolution_bitcast_fusion.3
  29.6 0.6 convolution_bitcast_fusion.2
  30.2 0.6 convolution_bitcast_fusion.1
  30.9 0.6 convolution_bitcast_fusion
  31.5 0.6 convolution_bitcast_fusion.8
  32.1 0.6 convolution_bitcast_fusion.7
  32.7 0.7 fusion.93
  33.4 0.7 fusion.92
  34.1 0.7 fusion.91
  34.9 0.7 fusion.90
  35.6 0.6 convolution_bitcast_fusion.4
  36.2 0.7 fusion.89
  36.9 0.7 fusion.88
  37.6 0.7 fusion.87
  38.3 0.7 fusion.86
  39.1 0.7 fusion.85
  39.8 0.7 fusion.84
  40.5 0.7 fusion.83
  41.2 0.7 fusion.82
  42.0 0.7 fusion.81
  42.7 0.7 fusion.80
  43.4 0.7 fusion.79
  44.1 0.7 fusion.78
  44.9 0.7 fusion.77
  45.6 0.7 fusion.76
  46.3 0.0 reduce-scatter.2.cloned.1.call-update
  46.3 1.1 pad.19
  47.5 0.4 copy.27
  47.9 0.1 slice.168
  48.1 12.9 %convolution_select_fusion = f32[4,32,8,3,256]{4,2,3,1,0:T(8,128)S(1)} fusion(bf16[3,3,3,256,256]{4,3,2,1,0:T(8,128)(2,1)S(1)} %copy-done, pred[8,3]{0,1:T(4,128)(4,1)S(1)} %copy-done.7, bf16[2,32,1,7,2,256]{5,3,4,1,0,2:T(8,128)(2,1)S(1)} %slice.168, bf16[2,32,1,8,3,256]{5,3,4,1,0,2:T(8,128)(2,1)S(1)} %copy.27), kind=kOutput, calls=%fused_computation.10 | convolution fusion | flops 5327290368 | bytes 7929880 | tf_op jit(solution)/shard_map/conv_general_dilated | solution.py:19
  61.0 0.1 slice.335
  61.1 0.2 copy.29
  61.3 1.6 %collective-permute-start.1 = (bf16[1,2,32,16,256]{4,2,3,1,0:T(8,128)(2,1)S(1)}, bf16[1,2,32,16,256]{4,2,3,1,0:T(8,128)(2,1)S(1)}, u32[]{:S(2)}, u32[]{:S(2)}) collective-permute-start(bf16[1,2,32,16,256]{4,2,3,1,0:T(8,128)(2,1)S(1)} %slice_bitcast_fusion.2), channel_id=1, source_target_pairs={{2,0},{4,2},{6,4},{8,6},{10,8},{12,10},{14,12},{3,1},{5,3},{7,5},{... | collective-permute-start | bytes 1572872 | tf_op jit(solution)/shard_map/ppermute | solution.py:10
  63.0 0.1 slice.169
  63.1 0.5 copy.28
  63.6 0.2 pad.17
  63.8 0.9 copy.22
  64.7 0.2 slice.166
  64.9 6.1 %fusion.9 = f32[2,32,8,3,256]{4,2,3,1,0:T(8,128)S(1)} fusion(bf16[3,3,3,256,256]{4,3,2,1,0:T(8,128)(2,1)S(1)} %copy-done, bf16[4,32,1,7,2,256]{5,3,4,1,0,2:T(8,128)(2,1)S(1)} %slice.166, bf16[4,32,1,8,3,256]{5,3,4,1,0,2:T(8,128)(2,1)S(1)} %copy.22, pred[8,3]{0,1:T(4,128)(4,1)S(1)} %copy-done.7), kind=kOutput, calls=%fused_computation.25 | convolution fusion | flops 5330829312 | bytes 7602200 | tf_op jit(solution)/shard_map/conv_general_dilated | solution.py:19
  71.1 0.5 copy.23
  71.6 5.2 %collective-permute-done.1 = bf16[1,2,32,16,256]{4,2,3,1,0:T(8,128)(2,1)S(1)} collective-permute-done((bf16[1,2,32,16,256]{4,2,3,1,0:T(8,128)(2,1)S(1)}, bf16[1,2,32,16,256]{4,2,3,1,0:T(8,128)(2,1)S(1)}, u32[]{:S(2)}, u32[]{:S(2)}) %collective-permute-start.1) | collective-permute-done | bytes 524320 | tf_op jit(solution)/shard_map/ppermute | solution.py:10
  76.8 0.8 fusion.36
  77.6 1.1 copy.41
  78.7 1.1 copy.40
  79.8 57.0 %reduce-scatter.2.cloned.1.call-done = f32[3,3,3,16,256]{4,3,2,1,0:T(8,128)} async-done(((f32[3,3,3,256,256]{4,3,2,1,0:T(8,128)}), f32[3,3,3,16,256]{4,3,2,1,0:T(8,128)}) %reduce-scatter.2.cloned.1.call-update) | async-done | bytes 442384 | tf_op jit(solution)/shard_map/reduce_scatter | solution.py:78
  136.7 1.8 %rev.4 = f32[3,3,3,16,256]{4,3,2,1,0:T(8,128)} reverse(f32[3,3,3,16,256]{4,3,2,1,0:T(8,128)} %reduce-scatter.2.cloned.1.call-done), dimensions={0} | reverse | bytes 884736 | tf_op jit(solution)/shard_map/rev | solution.py:78
  (17 shorter events, 0.1 us)
Async XLA Ops:
  7.2 40.9 %copy-start = (bf16[3,3,3,256,256]{4,3,2,1,0:T(8,128)(2,1)S(1)}, bf16[3,3,3,256,256]{4,3,2,1,0:T(8,128)(2,1)}, u32[]{:S(2)}) copy-start(bf16[3,3,3,256,256]{4,3,2,1,0:T(8,128)(2,1)} %param.4) | copy-start | bytes 10616836
  7.2 129.5 %reduce-scatter.2.cloned.1.call-start = ((), (), s32[]{:S(2)}) async-start(), calls=%async_computation.1 | async-start | bytes 7520256 | tf_op jit(solution)/shard_map/reduce_scatter | solution.py:78
  7.2 10.1 %copy-start.3 = (bf16[1,2,32,16,256]{4,3,2,1,0:T(8,128)(2,1)S(1)}, bf16[1,2,32,16,256]{4,3,2,1,0:T(8,128)(2,1)}, u32[]{:S(2)}) copy-start(bf16[1,2,32,16,256]{4,3,2,1,0:T(8,128)(2,1)} %param.5) | copy-start | bytes 1572868
  8.8 17.9 %collective-permute-start = (bf16[1,2,32,16,256]{4,2,3,1,0:T(8,128)(2,1)S(1)}, bf16[1,2,32,16,256]{4,2,3,1,0:T(8,128)(2,1)S(1)}, u32[]{:S(2)}, u32[]{:S(2)}) collective-permute-start(bf16[1,2,32,16,256]{4,2,3,1,0:T(8,128)(2,1)S(1)} %fusion.31), channel_id=1, source_target_pairs={{0,2},{2,4},{4,6},{6,8},{8,10},{10,12},{12,14},{1,3},{3,5},{5,7},{... | collective-permute-start | bytes 1572872 | tf_op jit(solution)/shard_map/ppermute | solution.py:10
  14.9 9.3 %copy-start.1 = (bf16[1,2,32,16,256]{4,2,3,1,0:T(8,128)(2,1)}, bf16[1,2,32,16,256]{4,2,3,1,0:T(8,128)(2,1)S(1)}, u32[]{:S(2)}) copy-start(bf16[1,2,32,16,256]{4,2,3,1,0:T(8,128)(2,1)S(1)} %copy.87) | copy-start | bytes 1572868
  18.4 2.2 %copy-start.5 = (bf16[1,2,32,16,256]{4,3,2,1,0:T(8,128)(2,1)S(1)}, bf16[1,2,32,16,256]{4,3,2,1,0:T(8,128)(2,1)}, u32[]{:S(2)}) copy-start(bf16[1,2,32,16,256]{4,3,2,1,0:T(8,128)(2,1)} %param.3) | copy-start | bytes 1572868
  46.3 1.7 %copy-start.7 = (pred[8,3]{0,1:T(4,128)(4,1)S(1)}, pred[8,3]{0,1:T(4,128)(4,1)}, u32[]{:S(2)}) copy-start(pred[8,3]{0,1:T(4,128)(4,1)} %constant.23) | copy-start | bytes 76
  61.3 2.3 %copy-start.2 = (bf16[4,32,1,16,256]{4,1,3,0,2:T(8,128)(2,1)S(1)}, bf16[4,32,1,16,256]{4,1,3,0,2:T(8,128)(2,1)}, u32[]{:S(2)}) copy-start(bf16[4,32,1,16,256]{4,1,3,0,2:T(8,128)(2,1)} %get-tuple-element.10) | copy-start | bytes 3145732
  61.3 15.4 %collective-permute-start.1 = (bf16[1,2,32,16,256]{4,2,3,1,0:T(8,128)(2,1)S(1)}, bf16[1,2,32,16,256]{4,2,3,1,0:T(8,128)(2,1)S(1)}, u32[]{:S(2)}, u32[]{:S(2)}) collective-permute-start(bf16[1,2,32,16,256]{4,2,3,1,0:T(8,128)(2,1)S(1)} %slice_bitcast_fusion.2), channel_id=1, source_target_pairs={{2,0},{4,2},{6,4},{8,6},{10,8},{12,10},{14,12},{3,1},{5,3},{7,5},{... | collective-permute-start | bytes 1572872 | tf_op jit(solution)/shard_map/ppermute | solution.py:10
  71.1 5.7 %copy-start.4 = (bf16[1,2,32,16,256]{4,3,2,1,0:T(8,128)(2,1)S(1)}, bf16[1,2,32,16,256]{4,3,2,1,0:T(8,128)(2,1)}, u32[]{:S(2)}) copy-start(bf16[1,2,32,16,256]{4,3,2,1,0:T(8,128)(2,1)} %param.5) | copy-start | bytes 1572868
  71.1 5.7 %copy-start.6 = (bf16[1,2,32,16,256]{4,3,2,1,0:T(8,128)(2,1)S(1)}, bf16[1,2,32,16,256]{4,3,2,1,0:T(8,128)(2,1)}, u32[]{:S(2)}) copy-start(bf16[1,2,32,16,256]{4,3,2,1,0:T(8,128)(2,1)} %param.3) | copy-start | bytes 1572868
Sparse Core Ops, SparseCore 0:
  46.5 90.2 reduce-scatter.1

commit v6 on v5

--- a/solution.py
+++ b/solution.py
@@ -51,10 +51,9 @@
             both = lax.dot_general(
                 window, shifted_grad, (((0,), (0,)), ((), ())), preferred_element_type=jnp.float32
             )
-            pieces[0, kh, kw] = both[:, :chans]
-            pieces[1, kh, kw] = both[:, chans:]
-    pieces = [pieces[kt, kh, kw] for kt in (2, 1, 0) for kh in range(3) for kw in range(3)]
-    return jnp.stack(pieces).reshape(3, 3, 3, chans, chans)
+            pieces[kh, kw] = jnp.concatenate([both, pieces[2, kh, kw]], axis=-1)
+    rows = [pieces[kh, kw] for kh in range(3) for kw in range(3)]
+    return jnp.stack(rows).reshape(3, 3, chans, 3, chans)
 
 
 def shards(clips, kernel, cotangent):
@@ -75,7 +74,8 @@
         cotangent.astype(jnp.float32) + grad_act * sig * (1.0 + wide * (1.0 - sig))
     ).astype(jnp.bfloat16)
     terms = kernel_terms(extended, act, cotangent)
-    grad_kernel = lax.rev(lax.psum_scatter(terms, ("tm", "dp"), scatter_dimension=3, tiled=True), (0,))
+    grad_kernel = lax.psum_scatter(terms, ("tm", "dp"), scatter_dimension=2, tiled=True)
+    grad_kernel = jnp.transpose(grad_kernel, (3, 0, 1, 2, 4))
     return (output, grad_input, grad_kernel)
 
 

time: 146 us -> 266 us (1.82)
  waiting for transfers between devices: 62.1 us -> 169 us
  local copies, waits for them, and re-layouts: 22.8 us -> 32.5 us
  other arithmetic: 3.48 us -> 12.9 us
  matrix products: 36 us -> 29.5 us
    unnamed x1 -> x2, waiting for transfers between devices: 0.02 us -> 149 us
    reduce_scatter x1 -> x0, waiting for transfers between devices: 57 us -> none  [shards(): lax.psum_scatter(terms, ('tm', 'dp'), scatter_dimension=3, tiled=True)]
    ppermute x2, waiting for transfers between devices: 5.16 us -> 19.3 us  [passed_along(): lax.ppermute(value, axis, [(source, source + steps) for source in range(l...]
    unnamed x37 -> x22, local copies, waits for them, and re-layouts: 16.8 us -> 5.97 us
    reshape x0 -> x1, local copies, waits for them, and re-layouts: none -> 10.7 us  [kernel_terms(): return jnp.stack(rows).reshape(3, 3, chans, 3, chans)]
    unnamed x0 -> x8, other arithmetic: none -> 7.55 us
    another operation x3, local copies, waits for them, and re-layouts: 0.98 us -> 8.27 us  [the longest x1 8.01 us: kernel_terms(): return jnp.stack(rows).reshape(3, 3, chans, 3, chans)]
    dot_general x9, matrix products: 11.6 us -> 4.98 us  [kernel_terms(): lax.dot_general(window, flat_grad, (((0,), (0,)), ((), ())), preferred_el...]
  transfers between devices with their start and end apart: 3 -> 3, of which waited for: 2 -> 3; matrix products, arithmetic and copies ran while one was open for 27% -> 14% of each run, Pallas kernels for 0% -> 0%
where the time goes in v6:
time: 266 us; the launch traced here: 265 us
  waiting for transfers between devices  169 us (64%)
  local copies, waits for them, and re-layouts  32.5 us (12%)
  matrix products  29.5 us (11%)
  between operations  15 us (6%)
  other arithmetic  12.9 us (5%)
  starting transfers between devices  6.51 us (2%)
    unnamed x2, waiting for transfers between devices  149 us
    ppermute x2, waiting for transfers between devices, passed_along(): lax.ppermute(value, axis, [(source, source + steps) for source in range(l...  19.3 us
    conv_general_dilated x2, matrix products, convolve(): lax.conv_general_dilated(source, kernel, (1, 1, 1), [time_pad, (1, 1), (1...  19.1 us
    reshape x1, local copies, waits for them, and re-layouts, kernel_terms(): return jnp.stack(rows).reshape(3, 3, chans, 3, chans)  10.7 us
    another operation x1, local copies, waits for them, and re-layouts, kernel_terms(): return jnp.stack(rows).reshape(3, 3, chans, 3, chans)  8.01 us
    unnamed x8, other arithmetic  7.55 us
    ppermute x2, starting transfers between devices, passed_along(): lax.ppermute(value, axis, [(source, source + steps) for source in range(l...  6.48 us
    unnamed x22, local copies, waits for them, and re-layouts  5.97 us
  transfers between devices with their start and end apart: 3, of which 3 were waited for; matrix products, arithmetic and copies ran while one was open for 14% of the time, Pallas kernels for 0%

profile of v6, /device:TPU:0, one launch (start us, length us, event | category | flops | bytes accessed | tf_op | source)
XLA Modules:
  0.0 265.1 jit_solution(3932747682216219419)
XLA Ops:
  7.2 0.0 copy-start
  7.2 0.0 all-reduce.6.cloned.1.call-start
  7.2 1.5 fusion.22
  8.8 5.1 %collective-permute-start = (bf16[1,2,32,16,256]{4,2,3,1,0:T(8,128)(2,1)S(1)}, bf16[1,2,32,16,256]{4,2,3,1,0:T(8,128)(2,1)S(1)}, u32[]{:S(2)}, u32[]{:S(2)}) collective-permute-start(bf16[1,2,32,16,256]{4,2,3,1,0:T(8,128)(2,1)S(1)} %fusion.22), channel_id=1, source_target_pairs={{0,2},{2,4},{4,6},{6,8},{8,10},{10,12},{12,14},{1,3},{3,5},{5,7},{... | collective-permute-start | bytes 1572872 | tf_op jit(solution)/shard_map/ppermute | solution.py:10
  13.8 1.2 copy.148
  15.0 0.0 copy-start.1
  15.1 1.7 convolution_bitcast_fusion.17
  16.7 0.4 convolution_bitcast_fusion.16
  17.2 0.4 convolution_bitcast_fusion.15
  17.6 0.4 convolution_bitcast_fusion.14
  18.0 0.4 convolution_bitcast_fusion.12
  18.4 0.4 convolution_bitcast_fusion.11
  18.8 0.4 convolution_bitcast_fusion.10
  19.3 0.2 pad_slice_fusion.11
  19.5 0.4 convolution_bitcast_fusion.9
  19.9 0.4 convolution_bitcast_fusion.13
  20.3 4.7 %collective-permute-done = bf16[1,2,32,16,256]{4,2,3,1,0:T(8,128)(2,1)S(1)} collective-permute-done((bf16[1,2,32,16,256]{4,2,3,1,0:T(8,128)(2,1)S(1)}, bf16[1,2,32,16,256]{4,2,3,1,0:T(8,128)(2,1)S(1)}, u32[]{:S(2)}, u32[]{:S(2)}) %collective-permute-start) | collective-permute-done | bytes 524320 | tf_op jit(solution)/shard_map/ppermute | solution.py:10
  25.0 1.1 pad_maximum_fusion
  26.1 0.6 convolution_bitcast_fusion.8
  26.7 0.6 convolution_bitcast_fusion.7
  27.3 0.6 convolution_bitcast_fusion.6
  27.9 0.6 convolution_bitcast_fusion.5
  28.5 0.6 convolution_bitcast_fusion.3
  29.1 0.6 convolution_bitcast_fusion.2
  29.8 0.6 convolution_bitcast_fusion.1
  30.4 0.6 convolution_bitcast_fusion
  31.0 1.0 fusion.49
  31.9 1.0 fusion.50
  32.9 0.9 fusion.51
  33.8 0.9 fusion.52
  34.8 0.6 convolution_bitcast_fusion.4
  35.4 1.0 fusion.53
  36.3 0.9 fusion.54
  37.3 1.0 fusion.55
  38.2 0.9 fusion.56
  39.1 0.9 fusion.57
  40.1 8.0 %copy.92 = f32[9,256,768]{1,2,0:T(8,128)} copy(f32[9,256,768]{2,1,0:T(8,128)} %fusion.57) | data formatting | bytes 14155776 | tf_op jit(solution)/shard_map/stack | solution.py:56
  48.1 10.7 %copy.93 = f32[3,3,256,3,256]{4,3,1,0,2:T(4,128)} copy(f32[3,3,256,3,256]{2,4,3,1,0:T(8,128)} %bitcast.193) | data formatting | bytes 14155776 | tf_op jit(solution)/shard_map/reshape | solution.py:56
  58.9 0.0 all-reduce.6.cloned.1.call-update
  58.9 0.0 copy-start.7
  58.9 1.1 pad.19
  60.0 0.4 copy.70
  60.5 0.1 slice.96
  60.6 12.9 %convolution_select_fusion = f32[4,32,8,3,256]{4,2,3,1,0:T(8,128)S(1)} fusion(bf16[3,3,3,256,256]{4,3,2,1,0:T(8,128)(2,1)S(1)} %copy-done, pred[8,3]{0,1:T(4,128)(4,1)S(1)} %copy-done.7, bf16[2,32,1,7,2,256]{5,3,4,1,0,2:T(8,128)(2,1)S(1)} %slice.96, bf16[2,32,1,8,3,256]{5,3,4,1,0,2:T(8,128)(2,1)S(1)} %copy.70), kind=kOutput, calls=%fused_computation.10 | convolution fusion | flops 5327290368 | bytes 7929880 | tf_op jit(solution)/shard_map/conv_general_dilated | solution.py:19
  73.6 0.1 slice.191
  73.7 0.2 copy.72
  73.8 0.8 slice_bitcast_fusion.2
  74.7 1.4 collective-permute-start.1
  76.1 0.1 slice.97
  76.2 1.7 copy.71
  77.9 0.6 dynamic-slice
  79.1 1.4 pad.17
  80.5 0.9 copy.65
  81.4 0.2 slice.94
  81.7 6.1 %fusion.9 = f32[2,32,8,3,256]{4,2,3,1,0:T(8,128)S(1)} fusion(bf16[3,3,3,256,256]{4,3,2,1,0:T(8,128)(2,1)S(1)} %copy-done, bf16[4,32,1,7,2,256]{5,3,4,1,0,2:T(8,128)(2,1)S(1)} %slice.94, bf16[4,32,1,8,3,256]{5,3,4,1,0,2:T(8,128)(2,1)S(1)} %copy.65, pred[8,3]{0,1:T(4,128)(4,1)S(1)} %copy-done.7), kind=kOutput, calls=%fused_computation.25 | convolution fusion | flops 5330829312 | bytes 7602200 | tf_op jit(solution)/shard_map/conv_general_dilated | solution.py:19
  87.9 0.0 copy-start.5
  87.9 0.5 copy.66
  88.3 14.6 %collective-permute-done.1 = bf16[1,2,32,16,256]{4,2,3,1,0:T(8,128)(2,1)} collective-permute-done((bf16[1,2,32,16,256]{4,2,3,1,0:T(8,128)(2,1)}, bf16[1,2,32,16,256]{4,2,3,1,0:T(8,128)(2,1)}, u32[]{:S(2)}, u32[]{:S(2)}) %collective-permute-start.1) | collective-permute-done | bytes 524320 | tf_op jit(solution)/shard_map/ppermute | solution.py:10
  103.0 1.8 fusion.27
  104.8 1.1 copy.94
  105.8 1.1 copy.95
  106.9 149.3 %all-reduce.6.cloned.1.call-done = f32[3,3,256,3,256]{4,3,1,0,2:T(4,128)} async-done(((f32[3,3,256,3,256]{4,3,1,0,2:T(4,128)}), f32[3,3,256,3,256]{4,3,1,0,2:T(4,128)}) %all-reduce.6.cloned.1.call-update) | async-done | bytes 7077904
  256.2 1.2 dynamic-slice_bitcast_fusion
  257.4 0.8 copy.96
  (12 shorter events, 0.0 us)
Async XLA Ops:
  7.2 53.4 %copy-start = (bf16[3,3,3,256,256]{4,3,2,1,0:T(8,128)(2,1)S(1)}, bf16[3,3,3,256,256]{4,3,2,1,0:T(8,128)(2,1)}, u32[]{:S(2)}) copy-start(bf16[3,3,3,256,256]{4,3,2,1,0:T(8,128)(2,1)} %param.4) | copy-start | bytes 10616836
  7.2 249.0 %all-reduce.6.cloned.1.call-start = ((), (), s32[]{:S(2)}) async-start(), calls=%async_computation | async-start | bytes 18874368
  8.8 8.0 %copy-start.3 = (bf16[1,2,32,16,256]{4,3,2,1,0:T(8,128)(2,1)S(1)}, bf16[1,2,32,16,256]{4,3,2,1,0:T(8,128)(2,1)}, u32[]{:S(2)}) copy-start(bf16[1,2,32,16,256]{4,3,2,1,0:T(8,128)(2,1)} %param.5) | copy-start | bytes 1572868
  8.8 16.2 %collective-permute-start = (bf16[1,2,32,16,256]{4,2,3,1,0:T(8,128)(2,1)S(1)}, bf16[1,2,32,16,256]{4,2,3,1,0:T(8,128)(2,1)S(1)}, u32[]{:S(2)}, u32[]{:S(2)}) collective-permute-start(bf16[1,2,32,16,256]{4,2,3,1,0:T(8,128)(2,1)S(1)} %fusion.22), channel_id=1, source_target_pairs={{0,2},{2,4},{4,6},{6,8},{8,10},{10,12},{12,14},{1,3},{3,5},{5,7},{... | collective-permute-start | bytes 1572872 | tf_op jit(solution)/shard_map/ppermute | solution.py:10
  15.0 4.2 %copy-start.1 = (bf16[1,2,32,16,256]{4,2,3,1,0:T(8,128)(2,1)}, bf16[1,2,32,16,256]{4,2,3,1,0:T(8,128)(2,1)S(1)}, u32[]{:S(2)}) copy-start(bf16[1,2,32,16,256]{4,2,3,1,0:T(8,128)(2,1)S(1)} %copy.148) | copy-start | bytes 1572868
  58.9 1.7 copy-start.7
  74.7 3.2 %copy-start.6 = (u32[32]{0:T(128)S(1)}, u32[32]{0:T(128)}, u32[]{:S(2)}) copy-start(u32[32]{0:T(128)} %constant.27) | copy-start | bytes 388
  74.7 28.3 %collective-permute-start.1 = (bf16[1,2,32,16,256]{4,2,3,1,0:T(8,128)(2,1)}, bf16[1,2,32,16,256]{4,2,3,1,0:T(8,128)(2,1)}, u32[]{:S(2)}, u32[]{:S(2)}) collective-permute-start(bf16[1,2,32,16,256]{4,2,3,1,0:T(8,128)(2,1)} %slice_bitcast_fusion.2), channel_id=1, source_target_pairs={{2,0},{4,2},{6,4},{8,6},{10,8},{12,10},{14,12},{3,1},{5,3},{7,5},{... | collective-permute-start | bytes 1572872 | tf_op jit(solution)/shard_map/ppermute | solution.py:10
  87.8 15.2 %copy-start.2 = (f32[2,32,8,3,256]{4,1,3,2,0:T(8,128)S(1)}, f32[2,32,8,3,256]{4,1,3,2,0:T(8,128)}, u32[]{:S(2)}) copy-start(f32[2,32,8,3,256]{4,1,3,2,0:T(8,128)} %copy.71) | copy-start | bytes 4718596
  87.8 15.1 %copy-start.4 = (bf16[1,2,32,16,256]{4,3,2,1,0:T(8,128)(2,1)S(1)}, bf16[1,2,32,16,256]{4,3,2,1,0:T(8,128)(2,1)}, u32[]{:S(2)}) copy-start(bf16[1,2,32,16,256]{4,3,2,1,0:T(8,128)(2,1)} %param.5) | copy-start | bytes 1572868
  87.9 15.1 %copy-start.5 = (bf16[1,2,32,16,256]{4,3,2,1,0:T(8,128)(2,1)S(1)}, bf16[1,2,32,16,256]{4,3,2,1,0:T(8,128)(2,1)}, u32[]{:S(2)}) copy-start(bf16[1,2,32,16,256]{4,3,2,1,0:T(8,128)(2,1)} %param.3) | copy-start | bytes 1572868
Sparse Core Ops, SparseCore 0:
  59.0 197.1 all-reduce.5
